TPU v7x, 32 devices: a whole 2x2x4 slice. The times are simulated.
32 devices in a mesh: sector: 8 (over y, x, core), sub: 4 (over z).
Axes of the slice: x: 2, y: 2, z: 4, core: 2. Of those that a mesh axis runs over, the one named last changes fastest.
Arguments:
- dual_load: float32 [8, 4, 2, 512, 256], P('sector', 'sub'), may hold values from -50 to 50
- flexibility: bfloat16 [8, 4, 2048, 2048], P('sector', 'sub'), may hold values from -10 to 10, as said below
- face_order: int32 [8, 4, 2048], P('sector', 'sub'), may hold values from 0 to 2047, each once within a row
- corner_index: int32 [8, 4, 32], P('sector', 'sub'), may hold values from 0 to 2047, as said below
- coarse_inverse: float32 [256, 256], replicated, may hold values from -10 to 10, as said below
Outputs:
- multiplier: float32 [8, 4, 2, 512, 256], P('sector', 'sub')
- residual: float32 [8, 4, 2, 512, 256], P('sector', 'sub')
Inputs may be any that keep to these rules, and one draw needn't show every extreme that they name: `flexibility`: a block of sizes of order one with a dominant diagonal; each subdomain's matrix is symmetric positive definite. `corner_index`: entries within one subdomain are distinct. `face_order`: each subdomain's row names every face slot once. `coarse_inverse`: symmetric positive definite with a dominant diagonal.
All inputs are finite; a program needn't handle non-finite values.
Results may differ from a plain program's by a relative error of at most 0.0087.
The roundings to bfloat16 on the way count: a program that leaves them out, or rounds other values in their place, can miss the bound.
Values may be sent and summed in bfloat16 or wider, within the bound.
No kernel may reach another device: no remote copies, remote signals or barrier semaphores. Data moves between devices by JAX's collectives and lax.ppermute only.
A program may use at most 128 MiB of HBM per device.

v0:
```python
import jax
import jax.numpy as jnp
from jax import lax
from jax.sharding import PartitionSpec as P

ITERS = 2


def passed_along(x, axis, by):
    count = lax.axis_size(axis)
    pairs = [(i, i + by) for i in range(count) if 0 <= i + by < count]
    return lax.ppermute(x, axis, pairs)


def from_behind(value, axis, steps):
    count = lax.axis_size(axis)
    pairs = [(source, (source + steps) % count) for source in range(count)]
    return lax.ppermute(value, axis, pairs)


def squares(residual):
    return lax.psum(jnp.sum(residual * residual, axis=(0, 1, 2, 3)), ("sector", "sub"))


def inner_sum(left, right):
    return jnp.sum(left * right, axis=(0, 1, 2, 3))


def shards(dual_load, flexibility, face_order, corner_index, coarse_inverse):
    slot_order = face_order[0, 0]
    corners = corner_index[0, 0]
    corner_count = corners.shape[0]
    matrix = jnp.take(jnp.take(flexibility[0, 0], slot_order, axis=0), slot_order, axis=1)
    face_width = slot_order.shape[0] // 4
    cases = dual_load.shape[-1]
    sub_count = lax.axis_size("sub")
    multiplier = jnp.zeros_like(dual_load)
    residual = dual_load
    direction = dual_load
    norm_now = squares(residual)
    for iteration in range(ITERS):
        rounded = direction[0, 0].astype(jnp.bfloat16)
        lower_sub = passed_along(rounded[0], "sub", 1)
        previous = from_behind(rounded[1], "sector", 1)
        face_stack = jnp.concatenate([-lower_sub, rounded[0], -previous, rounded[1]], axis=0)
        partial_value = jnp.take(face_stack, corners, axis=0).astype(jnp.float32)
        sector_total = lax.psum(partial_value.astype(jnp.bfloat16), "sub").astype(jnp.float32)
        sector_id = lax.axis_index("sector")
        everything = lax.all_gather(sector_total, "sector", axis=0, tiled=True)
        inverse_rows = lax.dynamic_slice_in_dim(
            coarse_inverse, sector_id * corner_count, corner_count, 0
        )
        coarse = jnp.dot(
            inverse_rows,
            everything,
            precision=lax.Precision.HIGHEST,
            preferred_element_type=jnp.float32,
        )
        coarse = coarse / sub_count
        correction = jnp.zeros((4 * face_width, cases), jnp.float32).at[corners].add(coarse)
        product = jnp.dot(matrix, face_stack, preferred_element_type=jnp.float32) + correction
        outgoing_sub = product[:face_width]
        outgoing_cycle = product[2 * face_width : 3 * face_width]
        upper_next = passed_along(outgoing_sub.astype(jnp.bfloat16), "sub", -1)
        cycle_next = from_behind(outgoing_cycle.astype(jnp.bfloat16), "sector", -1)
        own_sub = product[face_width : 2 * face_width]
        own_cycle = product[3 * face_width :]
        jump_pair = jnp.stack(
            [own_sub - upper_next.astype(jnp.float32), own_cycle - cycle_next.astype(jnp.float32)],
            axis=0,
        )
        image = jump_pair[None, None]
        curvature = lax.psum(inner_sum(direction, image), ("sector", "sub"))
        alpha = norm_now / curvature
        multiplier = multiplier + alpha * direction
        residual = residual - alpha * image
        if iteration + 1 < ITERS:
            norm_next = squares(residual)
            direction = residual + norm_next / norm_now * direction
            norm_now = norm_next
    return (multiplier, residual)


def solution(mesh):
    return jax.shard_map(
        shards,
        mesh=mesh,
        in_specs=(
            P("sector", "sub", None, None, None),
            P("sector", "sub", None, None),
            P("sector", "sub", None),
            P("sector", "sub", None),
            P(),
        ),
        out_specs=(P("sector", "sub", None, None, None), P("sector", "sub", None, None, None)),
        check_vma=False,
    )
```

profile of v0, /device:TPU:0, one launch (start us, length us, event | category | flops | bytes accessed | tf_op | source)
XLA Modules:
  0.0 299.5 jit_solution(9664023918029677284)
XLA Ops:
  0.7 1.3 convert_element_type.34
  2.1 0.5 collective-permute-start.1
  2.6 4.5 %collective-permute-start = (bf16[512,256]{1,0:T(8,128)(2,1)S(1)}, bf16[512,256]{1,0:T(8,128)(2,1)S(1)}, u32[]{:S(2)}, u32[]{:S(2)}) collective-permute-start(bf16[512,256]{1,0:T(8,128)(2,1)S(1)} %get-tuple-element.27), channel_id=1, source_target_pairs={{0,1},{1,2},{2,3},{4,5},{5,6},{6,7},{8,9},{9,10},{10,11},{12,13},{... | collective-permute-start | bytes 786440 | tf_op jit(solution)/shard_map/ppermute | solution.py:12
  7.2 20.8 %gather_fusion = bf16[2048,2048]{1,0:T(8,128)(2,1)} fusion(bf16[2048,2048]{1,0:T(8,128)(2,1)} %bitcast.51, s32[2048]{0:T(1024)S(1)} %broadcast_clamp_fusion), kind=kCustom, calls=%fused_computation.2 | custom fusion | bytes 16785408 | tf_op jit(solution)/shard_map/jit(_take)/gather | solution.py:33
  28.0 7.4 %broadcast_select_fusion = bf16[2048,2048]{1,0:T(8,128)(2,1)} fusion(bf16[2048,2048]{1,0:T(8,128)(2,1)} %gather_fusion, pred[2048]{0:T(1024)(128)(4,1)S(1)} %compare_and_fusion), kind=kLoop, calls=%fused_computation.6 | loop fusion | flops 4194304 | bytes 16779264 | tf_op jit(solution)/shard_map/jit(_take)/select_n | solution.py:33
  35.4 12.3 %copy.8 = bf16[2048,2048]{0,1:T(8,128)(2,1)} copy(bf16[2048,2048]{1,0:T(8,128)(2,1)} %broadcast_select_fusion) | data formatting | bytes 16777216 | tf_op jit(solution)/shard_map/jit(_take)/select_n | solution.py:33
  47.8 20.8 %gather_fusion.1 = bf16[2048,2048]{1,0:T(8,128)(2,1)} fusion(bf16[2048,2048]{0,1:T(8,128)(2,1)} %copy.8, s32[2048]{0:T(1024)S(1)} %broadcast_clamp_fusion), kind=kCustom, calls=%fused_computation.3 | custom fusion | bytes 16785408 | tf_op jit(solution)/shard_map/jit(_take)/gather | solution.py:33
  68.8 6.5 %fusion = f32[2048,256]{1,0:T(8,128)S(1)} fusion(bf16[2048,2048]{1,0:T(8,128)(2,1)} %gather_fusion.1, pred[2048]{0:T(1024)(128)(4,1)S(1)} %compare_and_fusion, bf16[512,256]{1,0:T(8,128)(2,1)} %copy-done.5, bf16[512,256]{1,0:T(8,128)(2,1)S(1)} %neg.13, bf16[512,256]{1,0:T(8,128)(2,1)} %copy-done.4, bf16[512,256]{1,0:T(8,128)(2,1)S(1)} %neg.12), kind=kOutput, calls=%fused_computation.8 | convolution fusion | flops 2155872256 | bytes 11536384 | tf_op jit(solution)/shard_map/dot_general | solution.py:61
  75.3 0.6 gather_fusion.2
  76.0 17.0 %psum.43 = bf16[32,256]{1,0:T(8,128)(2,1)S(1)} all-reduce(bf16[32,256]{1,0:T(8,128)(2,1)S(1)} %broadcast_select_fusion.5), channel_id=1, replica_groups=mesh['sector'=8,'sub'=4] {'sub'}, use_global_device_ids=true, to_apply=%region_2.4 | all-reduce | flops 8192 | bytes 32768 | tf_op jit(solution)/shard_map/psum | solution.py:47
  92.9 9.3 %all_gather.6 = f32[256,256]{1,0:T(8,128)S(1)} all-gather(f32[32,256]{1,0:T(8,128)S(1)} %convert_element_type.35), channel_id=1, replica_groups=mesh['sector'=8,'sub'=4] {'sector'}, dimensions={0}, use_global_device_ids=true | all-gather | bytes 294912 | tf_op jit(solution)/shard_map/all_gather | solution.py:49
  102.5 1.5 scatter_fusion
  104.2 1.2 copy-done.3
  105.4 1.4 collective-permute-start.2
  106.9 1.5 collective-permute-start.3
  108.3 7.7 %collective-permute-done.2 = bf16[512,256]{1,0:T(8,128)(2,1)S(1)} collective-permute-done((bf16[512,256]{1,0:T(8,128)(2,1)S(1)}, bf16[512,256]{1,0:T(8,128)(2,1)S(1)}, u32[]{:S(2)}, u32[]{:S(2)}) %collective-permute-start.2) | collective-permute-done | bytes 262176 | tf_op jit(solution)/shard_map/ppermute | solution.py:12
  116.0 1.4 fusion.9
  117.6 37.6 %all-reduce = (f32[256]{0:T(256)S(1)}, f32[256]{0:T(256)S(1)}) all-reduce(f32[256]{0:T(256)S(1)} %get-tuple-element.4, f32[256]{0:T(256)S(1)} %get-tuple-element.3), channel_id=1, replica_groups=mesh['sector'=8,'sub'=4] {'sector','sub'}, use_global_device_ids=true, to_apply=%region_1.2 | all-reduce | flops 512 | bytes 4096 | tf_op jit(solution)/shard_map/psum | solution.py:22
  155.5 41.7 %psum.45 = f32[256]{0:T(256)S(1)} all-reduce(f32[256]{0:T(256)S(1)} %multiply_reduce_fusion), channel_id=1, replica_groups=mesh['sector'=8,'sub'=4] {'sector','sub'}, use_global_device_ids=true, to_apply=%region_7.9 | all-reduce | flops 256 | bytes 2048 | tf_op jit(solution)/shard_map/psum | solution.py:22
  197.5 1.9 collective-permute-start.4
  199.3 4.8 %collective-permute-done.5 = bf16[512,256]{1,0:T(8,128)(2,1)S(1)} collective-permute-done((bf16[512,256]{1,0:T(8,128)(2,1)S(1)}, bf16[512,256]{1,0:T(8,128)(2,1)S(1)}, u32[]{:S(2)}, u32[]{:S(2)}) %collective-permute-start.5) | collective-permute-done | bytes 262176 | tf_op jit(solution)/shard_map/ppermute | solution.py:18
  204.6 7.8 %fusion.1 = f32[2048,256]{1,0:T(8,128)} fusion(bf16[2048,2048]{1,0:T(8,128)(2,1)} %gather_fusion.1, pred[2048]{0:T(1024)(128)(4,1)S(1)} %compare_and_fusion, bf16[512,256]{1,0:T(8,128)(2,1)S(1)} %get-tuple-element.26, bf16[512,256]{1,0:T(8,128)(2,1)S(1)} %neg.15, bf16[512,256]{1,0:T(8,128)(2,1)S(1)} %get-tuple-element.25, bf16[512,256]{1,0:T(8,128)(2,1)S(1)} %neg.14), kind=kOutput, calls=%fused_computation.9 | convolution fusion | flops 2155872256 | bytes 11536384 | tf_op jit(solution)/shard_map/dot_general | solution.py:61
  212.5 0.6 gather_fusion.3
  213.2 19.5 %psum.46 = bf16[32,256]{1,0:T(8,128)(2,1)S(1)} all-reduce(bf16[32,256]{1,0:T(8,128)(2,1)S(1)} %broadcast_select_fusion.4), channel_id=1, replica_groups=mesh['sector'=8,'sub'=4] {'sub'}, use_global_device_ids=true, to_apply=%region_8.10 | all-reduce | flops 8192 | bytes 32768 | tf_op jit(solution)/shard_map/psum | solution.py:47
  232.7 11.2 %all_gather.7 = f32[256,256]{1,0:T(8,128)S(1)} all-gather(f32[32,256]{1,0:T(8,128)S(1)} %convert_element_type.39), channel_id=1, replica_groups=mesh['sector'=8,'sub'=4] {'sector'}, dimensions={0}, use_global_device_ids=true | all-gather | bytes 294912 | tf_op jit(solution)/shard_map/all_gather | solution.py:49
  244.2 3.7 %scatter_fusion.1 = f32[2048,256]{1,0:T(8,128)} fusion(f32[2048,256]{1,0:T(8,128)} %fusion.1, s32[32]{0:T(128)S(1)} %fusion.19, f32[32,256]{1,0:T(8,128)S(1)} %convolution_multiply_fusion), kind=kCustom, calls=%fused_computation.5 | custom fusion | flops 8192 | bytes 98432 | tf_op jit(solution)/shard_map/scatter-add | solution.py:60
  247.9 1.8 convert.9
  249.8 1.3 collective-permute-start.6
  251.1 1.5 collective-permute-start.7
  252.5 7.7 %collective-permute-done.6 = bf16[512,256]{1,0:T(8,128)(2,1)S(1)} collective-permute-done((bf16[512,256]{1,0:T(8,128)(2,1)S(1)}, bf16[512,256]{1,0:T(8,128)(2,1)S(1)}, u32[]{:S(2)}, u32[]{:S(2)}) %collective-permute-start.6) | collective-permute-done | bytes 262176 | tf_op jit(solution)/shard_map/ppermute | solution.py:12
  260.6 37.2 %psum.47 = f32[256]{0:T(256)S(1)} all-reduce(f32[256]{0:T(256)S(1)} %fusion.6), channel_id=1, replica_groups=mesh['sector'=8,'sub'=4] {'sector','sub'}, use_global_device_ids=true, to_apply=%region_11.13 | all-reduce | flops 256 | bytes 2048 | tf_op jit(solution)/shard_map/psum | solution.py:73
  297.9 1.6 fusion.7
  (53 shorter events, 2.8 us)
Async XLA Ops:
  0.6 101.6 %copy-start = (f32[256,256]{1,0:T(8,128)S(1)}, f32[256,256]{1,0:T(8,128)}, u32[]{:S(2)}) copy-start(f32[256,256]{1,0:T(8,128)} %param.11) | copy-start | bytes 786436
  0.6 6.5 %copy-start.7 = (s32[1,1,32]{2,1,0:T(1,128)S(1)}, s32[1,1,32]{2,1,0:T(1,128)}, u32[]{:S(2)}) copy-start(s32[1,1,32]{2,1,0:T(1,128)} %param.10) | copy-start | bytes 388
  0.7 6.5 %copy-start.6 = (s32[1,1,2048]{2,1,0:T(1,128)S(1)}, s32[1,1,2048]{2,1,0:T(1,128)}, u32[]{:S(2)}) copy-start(s32[1,1,2048]{2,1,0:T(1,128)} %param.9) | copy-start | bytes 24580
  2.0 66.7 %copy-start.4 = (bf16[512,256]{1,0:T(8,128)(2,1)}, bf16[512,256]{1,0:T(8,128)(2,1)S(1)}, u32[]{:S(2)}) copy-start(bf16[512,256]{1,0:T(8,128)(2,1)S(1)} %get-tuple-element.27) | copy-start | bytes 786436
  2.0 66.7 %copy-start.5 = (bf16[512,256]{1,0:T(8,128)(2,1)}, bf16[512,256]{1,0:T(8,128)(2,1)S(1)}, u32[]{:S(2)}) copy-start(bf16[512,256]{1,0:T(8,128)(2,1)S(1)} %get-tuple-element.28) | copy-start | bytes 786436
  2.1 66.5 %collective-permute-start.1 = (bf16[512,256]{1,0:T(8,128)(2,1)S(1)}, bf16[512,256]{1,0:T(8,128)(2,1)S(1)}, u32[]{:S(2)}, u32[]{:S(2)}) collective-permute-start(bf16[512,256]{1,0:T(8,128)(2,1)S(1)} %get-tuple-element.28), channel_id=1, source_target_pairs={{0,4},{4,8},{8,12},{12,16},{16,20},{20,24},{24,28},{28,0},{1,5},{5... | collective-permute-start | bytes 786440 | tf_op jit(solution)/shard_map/ppermute | solution.py:18
  2.6 66.0 %collective-permute-start = (bf16[512,256]{1,0:T(8,128)(2,1)S(1)}, bf16[512,256]{1,0:T(8,128)(2,1)S(1)}, u32[]{:S(2)}, u32[]{:S(2)}) collective-permute-start(bf16[512,256]{1,0:T(8,128)(2,1)S(1)} %get-tuple-element.27), channel_id=1, source_target_pairs={{0,1},{1,2},{2,3},{4,5},{5,6},{6,7},{8,9},{9,10},{10,11},{12,13},{... | collective-permute-start | bytes 786440 | tf_op jit(solution)/shard_map/ppermute | solution.py:12
  104.1 1.4 copy-start.3
  105.4 11.9 %copy-start.1 = (f32[1,1,2,512,256]{4,3,2,1,0:T(8,128)S(1)}, f32[1,1,2,512,256]{4,3,2,1,0:T(8,128)}, u32[]{:S(2)}) copy-start(f32[1,1,2,512,256]{4,3,2,1,0:T(8,128)} %param.7) | copy-start | bytes 3145732
  105.4 10.6 %collective-permute-start.2 = (bf16[512,256]{1,0:T(8,128)(2,1)S(1)}, bf16[512,256]{1,0:T(8,128)(2,1)S(1)}, u32[]{:S(2)}, u32[]{:S(2)}) collective-permute-start(bf16[512,256]{1,0:T(8,128)(2,1)S(1)} %get-tuple-element.23), channel_id=1, source_target_pairs={{1,0},{2,1},{3,2},{5,4},{6,5},{7,6},{9,8},{10,9},{11,10},{13,12},{... | collective-permute-start | bytes 786440 | tf_op jit(solution)/shard_map/ppermute | solution.py:12
  106.9 9.2 %collective-permute-start.3 = (bf16[512,256]{1,0:T(8,128)(2,1)S(1)}, bf16[512,256]{1,0:T(8,128)(2,1)S(1)}, u32[]{:S(2)}, u32[]{:S(2)}) collective-permute-start(bf16[512,256]{1,0:T(8,128)(2,1)S(1)} %get-tuple-element.24), channel_id=1, source_target_pairs={{0,28},{4,0},{8,4},{12,8},{16,12},{20,16},{24,20},{28,24},{1,29},{... | collective-permute-start | bytes 786440 | tf_op jit(solution)/shard_map/ppermute | solution.py:18
  197.4 6.7 %collective-permute-start.5 = (bf16[512,256]{1,0:T(8,128)(2,1)S(1)}, bf16[512,256]{1,0:T(8,128)(2,1)S(1)}, u32[]{:S(2)}, u32[]{:S(2)}) collective-permute-start(bf16[512,256]{1,0:T(8,128)(2,1)S(1)} %get-tuple-element.26), channel_id=1, source_target_pairs={{0,4},{4,8},{8,12},{12,16},{16,20},{20,24},{24,28},{28,0},{1,5},{5... | collective-permute-start | bytes 786440 | tf_op jit(solution)/shard_map/ppermute | solution.py:18
  197.5 7.1 %collective-permute-start.4 = (bf16[512,256]{1,0:T(8,128)(2,1)S(1)}, bf16[512,256]{1,0:T(8,128)(2,1)S(1)}, u32[]{:S(2)}, u32[]{:S(2)}) collective-permute-start(bf16[512,256]{1,0:T(8,128)(2,1)S(1)} %get-tuple-element.25), channel_id=1, source_target_pairs={{0,1},{1,2},{2,3},{4,5},{5,6},{6,7},{8,9},{9,10},{10,11},{12,13},{... | collective-permute-start | bytes 786440 | tf_op jit(solution)/shard_map/ppermute | solution.py:12
  247.9 12.4 %copy-start.2 = (f32[2048,256]{1,0:T(8,128)S(1)}, f32[2048,256]{1,0:T(8,128)}, u32[]{:S(2)}) copy-start(f32[2048,256]{1,0:T(8,128)} %scatter_fusion.1) | copy-start | bytes 6291460
  249.8 10.5 %collective-permute-start.6 = (bf16[512,256]{1,0:T(8,128)(2,1)S(1)}, bf16[512,256]{1,0:T(8,128)(2,1)S(1)}, u32[]{:S(2)}, u32[]{:S(2)}) collective-permute-start(bf16[512,256]{1,0:T(8,128)(2,1)S(1)} %get-tuple-element.21), channel_id=1, source_target_pairs={{1,0},{2,1},{3,2},{5,4},{6,5},{7,6},{9,8},{10,9},{11,10},{13,12},{... | collective-permute-start | bytes 786440 | tf_op jit(solution)/shard_map/ppermute | solution.py:12
  251.1 9.2 %collective-permute-start.7 = (bf16[512,256]{1,0:T(8,128)(2,1)S(1)}, bf16[512,256]{1,0:T(8,128)(2,1)S(1)}, u32[]{:S(2)}, u32[]{:S(2)}) collective-permute-start(bf16[512,256]{1,0:T(8,128)(2,1)S(1)} %get-tuple-element.22), channel_id=1, source_target_pairs={{0,28},{4,0},{8,4},{12,8},{16,12},{20,16},{24,20},{28,24},{1,29},{... | collective-permute-start | bytes 786440 | tf_op jit(solution)/shard_map/ppermute | solution.py:18
where the time goes:
time: 301 us; the launch traced here: 300 us
  blocking collectives  174 us (58%)
  local copies, waits for them, and re-layouts  56.6 us (19%)
  waiting for transfers between devices  20.6 us (7%)
  other arithmetic  20.5 us (7%)
  matrix products  14.8 us (5%)
  starting transfers between devices  12.6 us (4%)
    psum x2, blocking collectives, squares(): lax.psum(jnp.sum(residual * residual, axis=(0, 1, 2, 3)), ('sector', 'sub'))  79.3 us
    psum x1, blocking collectives, shards(): curvature = lax.psum(inner_sum(direction, image), ('sector', 'sub'))  37.2 us
    psum x2, blocking collectives, shards(): lax.psum(partial_value.astype(jnp.bfloat16), 'sub').astype(jnp.float32)  36.5 us
    gather x1, local copies, waits for them, and re-layouts, shards(): jnp.take(flexibility[0, 0], slot_order, axis=0)  20.8 us
    gather x1, local copies, waits for them, and re-layouts, shards(): jnp.take(jnp.take(flexibility[0, 0], slot_order, axis=0), slot_order, axi...  20.8 us
    all_gather x2, blocking collectives, shards(): everything = lax.all_gather(sector_total, 'sector', axis=0, tiled=True)  20.5 us
    ppermute x4, waiting for transfers between devices, passed_along(): return lax.ppermute(x, axis, pairs)  15.8 us
    dot_general x2, matrix products, shards(): jnp.dot(matrix, face_stack, preferred_element_type=jnp.float32) + correction  14.3 us
  transfers between devices with their start and end apart: 8, of which 4 were waited for; matrix products, arithmetic and copies ran while one was open for 21% of the time, Pallas kernels for 0%

commit v1 on v0

--- a/solution.py
+++ b/solution.py
@@ -30,7 +30,9 @@
     slot_order = face_order[0, 0]
     corners = corner_index[0, 0]
     corner_count = corners.shape[0]
-    matrix = jnp.take(jnp.take(flexibility[0, 0], slot_order, axis=0), slot_order, axis=1)
+    slot_count = slot_order.shape[0]
+    own_place = jnp.zeros((slot_count,), jnp.int32).at[slot_order].set(jnp.arange(slot_count, dtype=jnp.int32))
+    matrix = flexibility[0, 0]
     face_width = slot_order.shape[0] // 4
     cases = dual_load.shape[-1]
     sub_count = lax.axis_size("sub")
@@ -58,7 +60,9 @@
         )
         coarse = coarse / sub_count
         correction = jnp.zeros((4 * face_width, cases), jnp.float32).at[corners].add(coarse)
-        product = jnp.dot(matrix, face_stack, preferred_element_type=jnp.float32) + correction
+        own_faces = jnp.take(face_stack, own_place, axis=0)
+        own_product = jnp.dot(matrix, own_faces, preferred_element_type=jnp.float32)
+        product = jnp.take(own_product, slot_order, axis=0) + correction
         outgoing_sub = product[:face_width]
         outgoing_cycle = product[2 * face_width : 3 * face_width]
         upper_next = passed_along(outgoing_sub.astype(jnp.bfloat16), "sub", -1)

time: 301 us -> 281 us (0.934)
  local copies, waits for them, and re-layouts: 56.6 us -> 45.5 us
  other arithmetic: 20.5 us -> 13.8 us
  blocking collectives: 174 us -> 170 us
    select_n x1 -> x0, local copies, waits for them, and re-layouts: 12.3 us -> none  [shards(): jnp.take(flexibility[0, 0], slot_order, axis=0)]
    gather x2 -> x4, local copies, waits for them, and re-layouts: 41.6 us -> 32.1 us  [the longest x2 17.1 us: shards(): product = jnp.take(own_product, slot_order, axis=0) + correction]
    scatter x0 -> x1, local copies, waits for them, and re-layouts: none -> 8.05 us  [shards(): jnp.zeros((slot_count,), jnp.int32).at[slot_order]]
    ppermute x4, waiting for transfers between devices: 15.8 us -> 20 us  [passed_along(): return lax.ppermute(x, axis, pairs)]
    dot_general x0 -> x2, local copies, waits for them, and re-layouts: none -> 3.84 us  [shards(): own_product = jnp.dot(matrix, own_faces, preferred_element_type=jnp.float32)]
    select_n x2 -> x3, other arithmetic: 7.45 us -> 3.86 us  [the longest x2 3.85 us: shards(): product = jnp.take(own_product, slot_order, axis=0) + correction]
  transfers between devices with their start and end apart: 8 -> 8, of which waited for: 4 -> 4; matrix products, arithmetic and copies ran while one was open for 21% -> 3% of each run, Pallas kernels for 0% -> 0%
where the time goes in v1:
time: 281 us
  blocking collectives  170 us (60%)
  local copies, waits for them, and re-layouts  45.5 us (16%)
  waiting for transfers between devices  22 us (8%)
  matrix products  15.5 us (6%)
  other arithmetic  13.8 us (5%)
  starting transfers between devices  12.7 us (5%)
    psum x2, blocking collectives, squares(): lax.psum(jnp.sum(residual * residual, axis=(0, 1, 2, 3)), ('sector', 'sub'))  79.2 us
    psum x1, blocking collectives, shards(): curvature = lax.psum(inner_sum(direction, image), ('sector', 'sub'))  37.4 us
    psum x2, blocking collectives, shards(): lax.psum(partial_value.astype(jnp.bfloat16), 'sub').astype(jnp.float32)  34.6 us
    ppermute x4, waiting for transfers between devices, passed_along(): return lax.ppermute(x, axis, pairs)  20 us
    all_gather x2, blocking collectives, shards(): everything = lax.all_gather(sector_total, 'sector', axis=0, tiled=True)  18.7 us
    gather x2, local copies, waits for them, and re-layouts, shards(): product = jnp.take(own_product, slot_order, axis=0) + correction  17.1 us
    dot_general x2, matrix products, shards(): own_product = jnp.dot(matrix, own_faces, preferred_element_type=jnp.float32)  15 us
    gather x2, local copies, waits for them, and re-layouts, shards(): own_faces = jnp.take(face_stack, own_place, axis=0)  15 us
  transfers between devices with their start and end apart: 8, of which 4 were waited for; matrix products, arithmetic and copies ran while one was open for 3% of the time, Pallas kernels for 0%

profile of v1, /device:TPU:0, one launch (start us, length us, event | category | flops | bytes accessed | tf_op | source)
XLA Modules:
  0.0 280.6 jit_solution(3341148262424951663)
XLA Ops:
  0.7 1.3 convert_element_type.34
  2.0 5.0 %collective-permute-start = (bf16[512,256]{1,0:T(8,128)(2,1)S(1)}, bf16[512,256]{1,0:T(8,128)(2,1)S(1)}, u32[]{:S(2)}, u32[]{:S(2)}) collective-permute-start(bf16[512,256]{1,0:T(8,128)(2,1)S(1)} %get-tuple-element.29), channel_id=1, source_target_pairs={{0,1},{1,2},{2,3},{4,5},{5,6},{6,7},{8,9},{9,10},{10,11},{12,13},{... | collective-permute-start | bytes 786440 | tf_op jit(solution)/shard_map/ppermute | solution.py:12
  7.2 8.0 %scatter_custom_fusion = s32[2048]{0:T(1024)S(1)} fusion(s32[2048]{0:T(1024)S(1)} %bitcast.66, s32[2048]{0:T(1024)S(1)} %iota.3, s32[]{:T(128)} %constant.11.clone.1), kind=kCustom, calls=%fused_computation.70 | custom fusion | bytes 8196 | tf_op jit(solution)/shard_map/scatter | solution.py:34
  16.1 7.5 %gather_fusion = bf16[2048,256]{1,0:T(8,128)(2,1)S(1)} fusion(bf16[2048,256]{1,0:T(8,128)(2,1)S(1)} %pad_maximum_fusion, s32[2048]{0:T(1024)S(1)} %fusion.33), kind=kCustom, calls=%fused_computation.clone | custom fusion | bytes 2105344 | tf_op jit(solution)/shard_map/jit(_take)/gather | solution.py:63
  23.7 17.1 %psum.43 = bf16[32,256]{1,0:T(8,128)(2,1)S(1)} all-reduce(bf16[32,256]{1,0:T(8,128)(2,1)S(1)} %broadcast_select_fusion.3), channel_id=1, replica_groups=mesh['sector'=8,'sub'=4] {'sub'}, use_global_device_ids=true, to_apply=%region_3.7 | all-reduce | flops 8192 | bytes 32768 | tf_op jit(solution)/shard_map/psum | solution.py:49
  40.8 9.3 %all_gather.6 = f32[256,256]{1,0:T(8,128)S(1)} all-gather(f32[32,256]{1,0:T(8,128)S(1)} %convert_element_type.35), channel_id=1, replica_groups=mesh['sector'=8,'sub'=4] {'sector'}, dimensions={0}, use_global_device_ids=true | all-gather | bytes 294912 | tf_op jit(solution)/shard_map/all_gather | solution.py:51
  50.2 7.5 %fusion.4 = f32[2048,256]{0,1:T(8,128)} fusion(bf16[1,1,2048,2048]{3,2,1,0:T(8,128)(2,1)} %param.12, bf16[2048,256]{1,0:T(8,128)(2,1)S(1)} %gather_fusion, pred[2048]{0:T(1024)(128)(4,1)S(1)} %compare_and_fusion.1), kind=kOutput, calls=%fused_computation.13 | convolution fusion | flops 2148007936 | bytes 11536384 | tf_op jit(solution)/shard_map/dot_general | solution.py:64
  57.7 1.9 copy.9
  59.6 8.6 %gather_fusion.1 = f32[2048,256]{1,0:T(8,128)} fusion(f32[2048,256]{1,0:T(8,128)S(1)} %copy.9, s32[2048]{0:T(1024)S(1)} %fusion.34), kind=kCustom, calls=%fused_computation.1.clone | custom fusion | bytes 4202496 | tf_op jit(solution)/shard_map/jit(_take)/gather | solution.py:65
  68.2 1.9 broadcast_select_fusion.1
  70.3 1.5 scatter_fusion
  72.1 1.4 collective-permute-start.2
  73.5 1.5 collective-permute-start.3
  75.0 7.7 %collective-permute-done.2 = bf16[512,256]{1,0:T(8,128)(2,1)S(1)} collective-permute-done((bf16[512,256]{1,0:T(8,128)(2,1)S(1)}, bf16[512,256]{1,0:T(8,128)(2,1)S(1)}, u32[]{:S(2)}, u32[]{:S(2)}) %collective-permute-start.2) | collective-permute-done | bytes 262176 | tf_op jit(solution)/shard_map/ppermute | solution.py:12
  84.0 37.5 %all-reduce = (f32[256]{0:T(256)S(1)}, f32[256]{0:T(256)S(1)}) all-reduce(f32[256]{0:T(256)S(1)} %get-tuple-element.6, f32[256]{0:T(256)S(1)} %get-tuple-element.4), channel_id=1, replica_groups=mesh['sector'=8,'sub'=4] {'sector','sub'}, use_global_device_ids=true, to_apply=%region_1.0 | all-reduce | flops 512 | bytes 4096 | tf_op jit(solution)/shard_map/psum | solution.py:22
  121.7 41.7 %psum.45 = f32[256]{0:T(256)S(1)} all-reduce(f32[256]{0:T(256)S(1)} %multiply_reduce_fusion), channel_id=1, replica_groups=mesh['sector'=8,'sub'=4] {'sector','sub'}, use_global_device_ids=true, to_apply=%region_8.12 | all-reduce | flops 256 | bytes 2048 | tf_op jit(solution)/shard_map/psum | solution.py:22
  163.7 1.9 collective-permute-start.4
  165.6 4.7 %collective-permute-done.4 = bf16[512,256]{1,0:T(8,128)(2,1)S(1)} collective-permute-done((bf16[512,256]{1,0:T(8,128)(2,1)S(1)}, bf16[512,256]{1,0:T(8,128)(2,1)S(1)}, u32[]{:S(2)}, u32[]{:S(2)}) %collective-permute-start.4) | collective-permute-done | bytes 262176 | tf_op jit(solution)/shard_map/ppermute | solution.py:12
  170.3 2.0 collective-permute-done.5
  173.0 7.5 %gather_fusion.3 = bf16[2048,256]{1,0:T(8,128)(2,1)S(1)} fusion(bf16[2048,256]{1,0:T(8,128)(2,1)S(1)} %pad_maximum_fusion.1, s32[2048]{0:T(1024)S(1)} %fusion.33), kind=kCustom, calls=%fused_computation.3.clone | custom fusion | bytes 2105344 | tf_op jit(solution)/shard_map/jit(_take)/gather | solution.py:63
  180.6 17.5 %psum.46 = bf16[32,256]{1,0:T(8,128)(2,1)S(1)} all-reduce(bf16[32,256]{1,0:T(8,128)(2,1)S(1)} %broadcast_select_fusion.2), channel_id=1, replica_groups=mesh['sector'=8,'sub'=4] {'sub'}, use_global_device_ids=true, to_apply=%region_9.13 | all-reduce | flops 8192 | bytes 32768 | tf_op jit(solution)/shard_map/psum | solution.py:49
  198.1 9.4 %all_gather.7 = f32[256,256]{1,0:T(8,128)S(1)} all-gather(f32[32,256]{1,0:T(8,128)S(1)} %convert_element_type.39), channel_id=1, replica_groups=mesh['sector'=8,'sub'=4] {'sector'}, dimensions={0}, use_global_device_ids=true | all-gather | bytes 294912 | tf_op jit(solution)/shard_map/all_gather | solution.py:51
  207.8 7.5 %fusion.7 = f32[2048,256]{0,1:T(8,128)} fusion(bf16[1,1,2048,2048]{3,2,1,0:T(8,128)(2,1)} %param.12, bf16[2048,256]{1,0:T(8,128)(2,1)S(1)} %gather_fusion.3, pred[2048]{0:T(1024)(128)(4,1)S(1)} %compare_and_fusion.1), kind=kOutput, calls=%fused_computation.14 | convolution fusion | flops 2148007936 | bytes 11536384 | tf_op jit(solution)/shard_map/dot_general | solution.py:64
  215.3 1.9 copy.10
  217.2 8.6 %gather_fusion.4 = f32[2048,256]{1,0:T(8,128)} fusion(f32[2048,256]{1,0:T(8,128)S(1)} %copy.10, s32[2048]{0:T(1024)S(1)} %fusion.34), kind=kCustom, calls=%fused_computation.4.clone | custom fusion | bytes 4202496 | tf_op jit(solution)/shard_map/jit(_take)/gather | solution.py:65
  225.8 1.9 broadcast_select_fusion
  227.7 1.5 scatter_fusion.1
  229.4 1.4 collective-permute-start.6
  230.9 1.5 collective-permute-start.7
  232.3 7.7 %collective-permute-done.6 = bf16[512,256]{1,0:T(8,128)(2,1)S(1)} collective-permute-done((bf16[512,256]{1,0:T(8,128)(2,1)S(1)}, bf16[512,256]{1,0:T(8,128)(2,1)S(1)}, u32[]{:S(2)}, u32[]{:S(2)}) %collective-permute-start.6) | collective-permute-done | bytes 262176 | tf_op jit(solution)/shard_map/ppermute | solution.py:12
  241.5 37.4 %psum.47 = f32[256]{0:T(256)S(1)} all-reduce(f32[256]{0:T(256)S(1)} %fusion.14), channel_id=1, replica_groups=mesh['sector'=8,'sub'=4] {'sector','sub'}, use_global_device_ids=true, to_apply=%region_12.16 | all-reduce | flops 256 | bytes 2048 | tf_op jit(solution)/shard_map/psum | solution.py:77
  278.9 1.6 fusion.15
  (69 shorter events, 6.0 us)
Async XLA Ops:
  0.6 69.5 %copy-start = (f32[256,256]{1,0:T(8,128)S(1)}, f32[256,256]{1,0:T(8,128)}, u32[]{:S(2)}) copy-start(f32[256,256]{1,0:T(8,128)} %param.15) | copy-start | bytes 786436
  0.6 6.4 %copy-start.11 = (s32[1,1,32]{2,1,0:T(1,128)S(1)}, s32[1,1,32]{2,1,0:T(1,128)}, u32[]{:S(2)}) copy-start(s32[1,1,32]{2,1,0:T(1,128)} %param.14) | copy-start | bytes 388
  0.7 6.5 %copy-start.10 = (s32[1,1,2048]{2,1,0:T(1,128)S(1)}, s32[1,1,2048]{2,1,0:T(1,128)}, u32[]{:S(2)}) copy-start(s32[1,1,2048]{2,1,0:T(1,128)} %param.13) | copy-start | bytes 24580
  2.0 13.3 %collective-permute-start = (bf16[512,256]{1,0:T(8,128)(2,1)S(1)}, bf16[512,256]{1,0:T(8,128)(2,1)S(1)}, u32[]{:S(2)}, u32[]{:S(2)}) collective-permute-start(bf16[512,256]{1,0:T(8,128)(2,1)S(1)} %get-tuple-element.29), channel_id=1, source_target_pairs={{0,1},{1,2},{2,3},{4,5},{5,6},{6,7},{8,9},{9,10},{10,11},{12,13},{... | collective-permute-start | bytes 786440 | tf_op jit(solution)/shard_map/ppermute | solution.py:12
  7.0 8.4 %collective-permute-start.1 = (bf16[512,256]{1,0:T(8,128)(2,1)S(1)}, bf16[512,256]{1,0:T(8,128)(2,1)S(1)}, u32[]{:S(2)}, u32[]{:S(2)}) collective-permute-start(bf16[512,256]{1,0:T(8,128)(2,1)S(1)} %get-tuple-element.30), channel_id=1, source_target_pairs={{0,4},{4,8},{8,12},{12,16},{16,20},{20,24},{24,28},{28,0},{1,5},{5... | collective-permute-start | bytes 786440 | tf_op jit(solution)/shard_map/ppermute | solution.py:18
  72.1 11.7 %copy-start.1 = (f32[1,1,2,512,256]{4,3,2,1,0:T(8,128)S(1)}, f32[1,1,2,512,256]{4,3,2,1,0:T(8,128)}, u32[]{:S(2)}) copy-start(f32[1,1,2,512,256]{4,3,2,1,0:T(8,128)} %param.11) | copy-start | bytes 3145732
  72.1 10.6 %collective-permute-start.2 = (bf16[512,256]{1,0:T(8,128)(2,1)S(1)}, bf16[512,256]{1,0:T(8,128)(2,1)S(1)}, u32[]{:S(2)}, u32[]{:S(2)}) collective-permute-start(bf16[512,256]{1,0:T(8,128)(2,1)S(1)} %get-tuple-element.25), channel_id=1, source_target_pairs={{1,0},{2,1},{3,2},{5,4},{6,5},{7,6},{9,8},{10,9},{11,10},{13,12},{... | collective-permute-start | bytes 786440 | tf_op jit(solution)/shard_map/ppermute | solution.py:12
  73.5 9.2 %collective-permute-start.3 = (bf16[512,256]{1,0:T(8,128)(2,1)S(1)}, bf16[512,256]{1,0:T(8,128)(2,1)S(1)}, u32[]{:S(2)}, u32[]{:S(2)}) collective-permute-start(bf16[512,256]{1,0:T(8,128)(2,1)S(1)} %get-tuple-element.26), channel_id=1, source_target_pairs={{0,28},{4,0},{8,4},{12,8},{16,12},{20,16},{24,20},{28,24},{1,29},{... | collective-permute-start | bytes 786440 | tf_op jit(solution)/shard_map/ppermute | solution.py:18
  83.8 37.7 %copy-start.2 = (f32[1,1,1,512,256]{4,3,2,1,0:T(8,128)S(1)}, f32[1,1,1,512,256]{4,3,2,1,0:T(8,128)}, u32[]{:S(2)}) copy-start(f32[1,1,1,512,256]{4,3,2,1,0:T(8,128)} %get-tuple-element.14) | copy-start | bytes 1572868
  83.8 37.7 %copy-start.5 = (f32[1,1,1,512,256]{4,3,2,1,0:T(8,128)S(1)}, f32[1,1,1,512,256]{4,3,2,1,0:T(8,128)}, u32[]{:S(2)}) copy-start(f32[1,1,1,512,256]{4,3,2,1,0:T(8,128)} %get-tuple-element.21) | copy-start | bytes 1572868
  163.7 6.6 %collective-permute-start.4 = (bf16[512,256]{1,0:T(8,128)(2,1)S(1)}, bf16[512,256]{1,0:T(8,128)(2,1)S(1)}, u32[]{:S(2)}, u32[]{:S(2)}) collective-permute-start(bf16[512,256]{1,0:T(8,128)(2,1)S(1)} %get-tuple-element.27), channel_id=1, source_target_pairs={{0,1},{1,2},{2,3},{4,5},{5,6},{6,7},{8,9},{9,10},{10,11},{12,13},{... | collective-permute-start | bytes 786440 | tf_op jit(solution)/shard_map/ppermute | solution.py:12
  165.5 6.7 %collective-permute-start.5 = (bf16[512,256]{1,0:T(8,128)(2,1)S(1)}, bf16[512,256]{1,0:T(8,128)(2,1)S(1)}, u32[]{:S(2)}, u32[]{:S(2)}) collective-permute-start(bf16[512,256]{1,0:T(8,128)(2,1)S(1)} %get-tuple-element.28), channel_id=1, source_target_pairs={{0,4},{4,8},{8,12},{12,16},{16,20},{20,24},{24,28},{28,0},{1,5},{5... | collective-permute-start | bytes 786440 | tf_op jit(solution)/shard_map/ppermute | solution.py:18
  229.4 11.8 %copy-start.3 = (f32[1,1,1,512,256]{4,3,2,1,0:T(8,128)S(1)}, f32[1,1,1,512,256]{4,3,2,1,0:T(8,128)}, u32[]{:S(2)}) copy-start(f32[1,1,1,512,256]{4,3,2,1,0:T(8,128)} %get-tuple-element.14) | copy-start | bytes 1572868
  229.4 11.8 %copy-start.6 = (f32[1,1,1,512,256]{4,3,2,1,0:T(8,128)S(1)}, f32[1,1,1,512,256]{4,3,2,1,0:T(8,128)}, u32[]{:S(2)}) copy-start(f32[1,1,1,512,256]{4,3,2,1,0:T(8,128)} %get-tuple-element.21) | copy-start | bytes 1572868
  229.4 10.6 %collective-permute-start.6 = (bf16[512,256]{1,0:T(8,128)(2,1)S(1)}, bf16[512,256]{1,0:T(8,128)(2,1)S(1)}, u32[]{:S(2)}, u32[]{:S(2)}) collective-permute-start(bf16[512,256]{1,0:T(8,128)(2,1)S(1)} %get-tuple-element.23), channel_id=1, source_target_pairs={{1,0},{2,1},{3,2},{5,4},{6,5},{7,6},{9,8},{10,9},{11,10},{13,12},{... | collective-permute-start | bytes 786440 | tf_op jit(solution)/shard_map/ppermute | solution.py:12
  230.9 9.2 %collective-permute-start.7 = (bf16[512,256]{1,0:T(8,128)(2,1)S(1)}, bf16[512,256]{1,0:T(8,128)(2,1)S(1)}, u32[]{:S(2)}, u32[]{:S(2)}) collective-permute-start(bf16[512,256]{1,0:T(8,128)(2,1)S(1)} %get-tuple-element.24), channel_id=1, source_target_pairs={{0,28},{4,0},{8,4},{12,8},{16,12},{20,16},{24,20},{28,24},{1,29},{... | collective-permute-start | bytes 786440 | tf_op jit(solution)/shard_map/ppermute | solution.py:18
  241.2 37.7 %copy-start.4 = (f32[1,1,1,512,256]{4,3,2,1,0:T(8,128)S(1)}, f32[1,1,1,512,256]{4,3,2,1,0:T(8,128)}, u32[]{:S(2)}) copy-start(f32[1,1,1,512,256]{4,3,2,1,0:T(8,128)} %get-tuple-element.14) | copy-start | bytes 1572868
  241.2 37.7 %copy-start.7 = (f32[1,1,1,512,256]{4,3,2,1,0:T(8,128)S(1)}, f32[1,1,1,512,256]{4,3,2,1,0:T(8,128)}, u32[]{:S(2)}) copy-start(f32[1,1,1,512,256]{4,3,2,1,0:T(8,128)} %get-tuple-element.21) | copy-start | bytes 1572868
  241.2 37.7 %copy-start.8 = (f32[1,1,1,512,256]{4,3,2,1,0:T(8,128)S(1)}, f32[1,1,1,512,256]{4,3,2,1,0:T(8,128)}, u32[]{:S(2)}) copy-start(f32[1,1,1,512,256]{4,3,2,1,0:T(8,128)} %get-tuple-element.9) | copy-start | bytes 1572868
  241.2 37.7 %copy-start.9 = (f32[1,1,1,512,256]{4,3,2,1,0:T(8,128)S(1)}, f32[1,1,1,512,256]{4,3,2,1,0:T(8,128)}, u32[]{:S(2)}) copy-start(f32[1,1,1,512,256]{4,3,2,1,0:T(8,128)} %get-tuple-element.20) | copy-start | bytes 1572868

commit v2 on v1

--- a/solution.py
+++ b/solution.py
@@ -18,8 +18,21 @@
     return lax.ppermute(value, axis, pairs)
 
 
+def total(x):
+    for axis in ("sub", "sector"):
+        count = lax.axis_size(axis)
+        if count & (count - 1):
+            x = lax.psum(x, axis)
+            continue
+        step = 1
+        while step < count:
+            x = x + lax.ppermute(x, axis, [(i, i ^ step) for i in range(count)])
+            step *= 2
+    return x
+
+
 def squares(residual):
-    return lax.psum(jnp.sum(residual * residual, axis=(0, 1, 2, 3)), ("sector", "sub"))
+    return total(jnp.sum(residual * residual, axis=(0, 1, 2, 3)))
 
 
 def inner_sum(left, right):
@@ -39,7 +52,6 @@
     multiplier = jnp.zeros_like(dual_load)
     residual = dual_load
     direction = dual_load
-    norm_now = squares(residual)
     for iteration in range(ITERS):
         rounded = direction[0, 0].astype(jnp.bfloat16)
         lower_sub = passed_along(rounded[0], "sub", 1)
@@ -74,7 +86,11 @@
             axis=0,
         )
         image = jump_pair[None, None]
-        curvature = lax.psum(inner_sum(direction, image), ("sector", "sub"))
+        if iteration == 0:
+            both = total(jnp.stack([inner_sum(residual, residual), inner_sum(direction, image)]))
+            norm_now, curvature = both[0], both[1]
+        else:
+            curvature = total(inner_sum(direction, image))
         alpha = norm_now / curvature
         multiplier = multiplier + alpha * direction
         residual = residual - alpha * image

time: 281 us -> 211 us (0.75)
  blocking collectives: 170 us -> 51.9 us
  waiting for transfers between devices: 22 us -> 63.9 us
  starting transfers between devices: 12.7 us -> 20.3 us
    psum x3 -> x0, blocking collectives: 117 us -> none  [the longest x2 79.2 us: squares(): lax.psum(jnp.sum(residual * residual, axis=(0, 1, 2, 3)), ('sector', 'sub'))]
    ppermute x0 -> x15, waiting for transfers between devices: none -> 41.9 us  [total(): x = x + lax.ppermute(x, axis, [(i, i ^ step) for i in range(count)])]
    ppermute x0 -> x15, starting transfers between devices: none -> 7.45 us  [total(): x = x + lax.ppermute(x, axis, [(i, i ^ step) for i in range(count)])]
  transfers between devices with their start and end apart: 8 -> 23, of which waited for: 4 -> 19; matrix products, arithmetic and copies ran while one was open for 3% -> 4% of each run, Pallas kernels for 0% -> 0%
where the time goes in v2:
time: 211 us; the launch traced here: 210 us
  waiting for transfers between devices  63.9 us (30%)
  blocking collectives  51.9 us (25%)
  local copies, waits for them, and re-layouts  45.5 us (22%)
  starting transfers between devices  20.3 us (10%)
  matrix products  15.4 us (7%)
  other arithmetic  12 us (6%)
    ppermute x15, waiting for transfers between devices, total(): x = x + lax.ppermute(x, axis, [(i, i ^ step) for i in range(count)])  41.9 us
    psum x2, blocking collectives, shards(): lax.psum(partial_value.astype(jnp.bfloat16), 'sub').astype(jnp.float32)  33.1 us
    ppermute x4, waiting for transfers between devices, passed_along(): return lax.ppermute(x, axis, pairs)  19.2 us
    all_gather x2, blocking collectives, shards(): everything = lax.all_gather(sector_total, 'sector', axis=0, tiled=True)  18.8 us
    gather x2, local copies, waits for them, and re-layouts, shards(): product = jnp.take(own_product, slot_order, axis=0) + correction  17.1 us
    gather x2, local copies, waits for them, and re-layouts, shards(): own_faces = jnp.take(face_stack, own_place, axis=0)  15 us
    dot_general x2, matrix products, shards(): own_product = jnp.dot(matrix, own_faces, preferred_element_type=jnp.float32)  15 us
    ppermute x4, starting transfers between devices, passed_along(): return lax.ppermute(x, axis, pairs)  9.75 us
  transfers between devices with their start and end apart: 23, of which 19 were waited for; matrix products, arithmetic and copies ran while one was open for 4% of the time, Pallas kernels for 0%

profile of v2, /device:TPU:0, one launch (start us, length us, event | category | flops | bytes accessed | tf_op | source)
XLA Modules:
  0.0 210.2 jit_solution(8460583549095076116)
XLA Ops:
  2.0 5.0 %collective-permute-start = (bf16[512,256]{1,0:T(8,128)(2,1)S(1)}, bf16[512,256]{1,0:T(8,128)(2,1)S(1)}, u32[]{:S(2)}, u32[]{:S(2)}) collective-permute-start(bf16[512,256]{1,0:T(8,128)(2,1)S(1)} %get-tuple-element.29), channel_id=1, source_target_pairs={{0,1},{1,2},{2,3},{4,5},{5,6},{6,7},{8,9},{9,10},{10,11},{12,13},{... | collective-permute-start | bytes 786440 | tf_op jit(solution)/shard_map/ppermute | solution.py:12
  7.2 8.0 %scatter_custom_fusion = s32[2048]{0:T(1024)S(1)} fusion(s32[2048]{0:T(1024)S(1)} %bitcast.78, s32[2048]{0:T(1024)S(1)} %iota.3, s32[]{:T(128)} %constant.11.clone.1), kind=kCustom, calls=%fused_computation.70 | custom fusion | bytes 8196 | tf_op jit(solution)/shard_map/scatter | solution.py:47
  16.1 7.5 %gather_fusion = bf16[2048,256]{1,0:T(8,128)(2,1)S(1)} fusion(bf16[2048,256]{1,0:T(8,128)(2,1)S(1)} %pad_maximum_fusion, s32[2048]{0:T(1024)S(1)} %fusion.33), kind=kCustom, calls=%fused_computation.clone | custom fusion | bytes 2105344 | tf_op jit(solution)/shard_map/jit(_take)/gather | solution.py:75
  23.7 17.1 %psum.14 = bf16[32,256]{1,0:T(8,128)(2,1)S(1)} all-reduce(bf16[32,256]{1,0:T(8,128)(2,1)S(1)} %broadcast_select_fusion.3), channel_id=1, replica_groups=mesh['sector'=8,'sub'=4] {'sub'}, use_global_device_ids=true, to_apply=%region_2.6 | all-reduce | flops 8192 | bytes 32768 | tf_op jit(solution)/shard_map/psum | solution.py:61
  40.8 9.3 %all_gather.6 = f32[256,256]{1,0:T(8,128)S(1)} all-gather(f32[32,256]{1,0:T(8,128)S(1)} %convert_element_type.35), channel_id=1, replica_groups=mesh['sector'=8,'sub'=4] {'sector'}, dimensions={0}, use_global_device_ids=true | all-gather | bytes 294912 | tf_op jit(solution)/shard_map/all_gather | solution.py:63
  50.2 7.5 %fusion.4 = f32[2048,256]{0,1:T(8,128)} fusion(bf16[1,1,2048,2048]{3,2,1,0:T(8,128)(2,1)} %param.12, bf16[2048,256]{1,0:T(8,128)(2,1)S(1)} %gather_fusion, pred[2048]{0:T(1024)(128)(4,1)S(1)} %compare_and_fusion.1), kind=kOutput, calls=%fused_computation.13 | convolution fusion | flops 2148007936 | bytes 11536384 | tf_op jit(solution)/shard_map/dot_general | solution.py:76
  57.6 1.9 copy.9
  59.6 8.6 %gather_fusion.1 = f32[2048,256]{1,0:T(8,128)} fusion(f32[2048,256]{1,0:T(8,128)S(1)} %copy.9, s32[2048]{0:T(1024)S(1)} %fusion.34), kind=kCustom, calls=%fused_computation.1.clone | custom fusion | bytes 4202496 | tf_op jit(solution)/shard_map/jit(_take)/gather | solution.py:77
  68.1 1.9 broadcast_select_fusion.1
  74.9 7.7 %collective-permute-done.2 = bf16[512,256]{1,0:T(8,128)(2,1)S(1)} collective-permute-done((bf16[512,256]{1,0:T(8,128)(2,1)S(1)}, bf16[512,256]{1,0:T(8,128)(2,1)S(1)}, u32[]{:S(2)}, u32[]{:S(2)}) %collective-permute-start.2) | collective-permute-done | bytes 262176 | tf_op jit(solution)/shard_map/ppermute | solution.py:12
  83.2 3.6 %collective-permute-done.4 = f32[2,256]{1,0:T(2,128)S(1)} collective-permute-done((f32[2,256]{1,0:T(2,128)S(1)}, f32[2,256]{1,0:T(2,128)S(1)}, u32[]{:S(2)}, u32[]{:S(2)}) %collective-permute-start.4) | collective-permute-done | bytes 2080 | tf_op jit(solution)/shard_map/ppermute | solution.py:29
  86.8 4.5 %collective-permute-done.5 = f32[2,256]{1,0:T(2,128)S(1)} collective-permute-done((f32[2,256]{1,0:T(2,128)S(1)}, f32[2,256]{1,0:T(2,128)S(1)}, u32[]{:S(2)}, u32[]{:S(2)}) %collective-permute-start.5) | collective-permute-done | bytes 2080 | tf_op jit(solution)/shard_map/ppermute | solution.py:29
  94.1 2.1 collective-permute-done.7
  97.6 2.1 collective-permute-done.8
  100.0 3.6 %collective-permute-done.9 = f32[256]{0:T(256)S(1)} collective-permute-done((f32[256]{0:T(256)S(1)}, f32[256]{0:T(256)S(1)}, u32[]{:S(2)}, u32[]{:S(2)}) %collective-permute-start.9) | collective-permute-done | bytes 1056 | tf_op jit(solution)/shard_map/ppermute | solution.py:29
  103.6 4.5 %collective-permute-done.10 = f32[256]{0:T(256)S(1)} collective-permute-done((f32[256]{0:T(256)S(1)}, f32[256]{0:T(256)S(1)}, u32[]{:S(2)}, u32[]{:S(2)}) %collective-permute-start.10) | collective-permute-done | bytes 1056 | tf_op jit(solution)/shard_map/ppermute | solution.py:29
  110.8 2.0 collective-permute-done.12
  114.3 2.0 collective-permute-done.13
  116.6 1.9 collective-permute-start.14
  118.6 3.8 %collective-permute-done.14 = bf16[512,256]{1,0:T(8,128)(2,1)S(1)} collective-permute-done((bf16[512,256]{1,0:T(8,128)(2,1)S(1)}, bf16[512,256]{1,0:T(8,128)(2,1)S(1)}, u32[]{:S(2)}, u32[]{:S(2)}) %collective-permute-start.14) | collective-permute-done | bytes 262176 | tf_op jit(solution)/shard_map/ppermute | solution.py:12
  122.5 2.8 %collective-permute-done.15 = bf16[512,256]{1,0:T(8,128)(2,1)S(1)} collective-permute-done((bf16[512,256]{1,0:T(8,128)(2,1)S(1)}, bf16[512,256]{1,0:T(8,128)(2,1)S(1)}, u32[]{:S(2)}, u32[]{:S(2)}) %collective-permute-start.15) | collective-permute-done | bytes 262176 | tf_op jit(solution)/shard_map/ppermute | solution.py:18
  126.1 7.5 %gather_fusion.3 = bf16[2048,256]{1,0:T(8,128)(2,1)S(1)} fusion(bf16[2048,256]{1,0:T(8,128)(2,1)S(1)} %pad_maximum_fusion.1, s32[2048]{0:T(1024)S(1)} %fusion.33), kind=kCustom, calls=%fused_computation.3.clone | custom fusion | bytes 2105344 | tf_op jit(solution)/shard_map/jit(_take)/gather | solution.py:75
  133.7 15.9 %psum.15 = bf16[32,256]{1,0:T(8,128)(2,1)S(1)} all-reduce(bf16[32,256]{1,0:T(8,128)(2,1)S(1)} %broadcast_select_fusion.2), channel_id=1, replica_groups=mesh['sector'=8,'sub'=4] {'sub'}, use_global_device_ids=true, to_apply=%region_6.10 | all-reduce | flops 8192 | bytes 32768 | tf_op jit(solution)/shard_map/psum | solution.py:61
  149.6 9.5 %all_gather.7 = f32[256,256]{1,0:T(8,128)S(1)} all-gather(f32[32,256]{1,0:T(8,128)S(1)} %convert_element_type.39), channel_id=1, replica_groups=mesh['sector'=8,'sub'=4] {'sector'}, dimensions={0}, use_global_device_ids=true | all-gather | bytes 294912 | tf_op jit(solution)/shard_map/all_gather | solution.py:63
  159.3 7.5 %fusion.7 = f32[2048,256]{0,1:T(8,128)} fusion(bf16[1,1,2048,2048]{3,2,1,0:T(8,128)(2,1)} %param.12, bf16[2048,256]{1,0:T(8,128)(2,1)S(1)} %gather_fusion.3, pred[2048]{0:T(1024)(128)(4,1)S(1)} %compare_and_fusion.1), kind=kOutput, calls=%fused_computation.14 | convolution fusion | flops 2148007936 | bytes 11536384 | tf_op jit(solution)/shard_map/dot_general | solution.py:76
  168.8 8.6 %gather_fusion.4 = f32[2048,256]{1,0:T(8,128)} fusion(f32[2048,256]{1,0:T(8,128)S(1)} %copy.10, s32[2048]{0:T(1024)S(1)} %fusion.34), kind=kCustom, calls=%fused_computation.4.clone | custom fusion | bytes 4202496 | tf_op jit(solution)/shard_map/jit(_take)/gather | solution.py:77
  177.3 1.9 broadcast_select_fusion
  183.9 7.7 %collective-permute-done.16 = bf16[512,256]{1,0:T(8,128)(2,1)S(1)} collective-permute-done((bf16[512,256]{1,0:T(8,128)(2,1)S(1)}, bf16[512,256]{1,0:T(8,128)(2,1)S(1)}, u32[]{:S(2)}, u32[]{:S(2)}) %collective-permute-start.16) | collective-permute-done | bytes 262176 | tf_op jit(solution)/shard_map/ppermute | solution.py:12
  192.1 3.6 %collective-permute-done.18 = f32[256]{0:T(256)S(1)} collective-permute-done((f32[256]{0:T(256)S(1)}, f32[256]{0:T(256)S(1)}, u32[]{:S(2)}, u32[]{:S(2)}) %collective-permute-start.18) | collective-permute-done | bytes 1056 | tf_op jit(solution)/shard_map/ppermute | solution.py:29
  195.7 4.5 %collective-permute-done.19 = f32[256]{0:T(256)S(1)} collective-permute-done((f32[256]{0:T(256)S(1)}, f32[256]{0:T(256)S(1)}, u32[]{:S(2)}, u32[]{:S(2)}) %collective-permute-start.19) | collective-permute-done | bytes 1056 | tf_op jit(solution)/shard_map/ppermute | solution.py:29
  201.8 3.1 %collective-permute-done.21 = f32[256]{0:T(256)S(1)} collective-permute-done((f32[256]{0:T(256)S(1)}, f32[256]{0:T(256)S(1)}, u32[]{:S(2)}, u32[]{:S(2)}) %collective-permute-start.21) | collective-permute-done | bytes 1056 | tf_op jit(solution)/shard_map/ppermute | solution.py:29
  205.4 3.1 %collective-permute-done.22 = f32[256]{0:T(256)S(1)} collective-permute-done((f32[256]{0:T(256)S(1)}, f32[256]{0:T(256)S(1)}, u32[]{:S(2)}, u32[]{:S(2)}) %collective-permute-start.22) | collective-permute-done | bytes 1056 | tf_op jit(solution)/shard_map/ppermute | solution.py:29
  (103 shorter events, 28.9 us)
Async XLA Ops:
  0.6 69.4 %copy-start = (f32[256,256]{1,0:T(8,128)S(1)}, f32[256,256]{1,0:T(8,128)}, u32[]{:S(2)}) copy-start(f32[256,256]{1,0:T(8,128)} %param.15) | copy-start | bytes 786436
  0.6 6.4 %copy-start.7 = (s32[1,1,32]{2,1,0:T(1,128)S(1)}, s32[1,1,32]{2,1,0:T(1,128)}, u32[]{:S(2)}) copy-start(s32[1,1,32]{2,1,0:T(1,128)} %param.14) | copy-start | bytes 388
  0.7 6.5 %copy-start.6 = (s32[1,1,2048]{2,1,0:T(1,128)S(1)}, s32[1,1,2048]{2,1,0:T(1,128)}, u32[]{:S(2)}) copy-start(s32[1,1,2048]{2,1,0:T(1,128)} %param.13) | copy-start | bytes 24580
  2.0 13.3 %collective-permute-start = (bf16[512,256]{1,0:T(8,128)(2,1)S(1)}, bf16[512,256]{1,0:T(8,128)(2,1)S(1)}, u32[]{:S(2)}, u32[]{:S(2)}) collective-permute-start(bf16[512,256]{1,0:T(8,128)(2,1)S(1)} %get-tuple-element.29), channel_id=1, source_target_pairs={{0,1},{1,2},{2,3},{4,5},{5,6},{6,7},{8,9},{9,10},{10,11},{12,13},{... | collective-permute-start | bytes 786440 | tf_op jit(solution)/shard_map/ppermute | solution.py:12
  7.0 8.4 %collective-permute-start.1 = (bf16[512,256]{1,0:T(8,128)(2,1)S(1)}, bf16[512,256]{1,0:T(8,128)(2,1)S(1)}, u32[]{:S(2)}, u32[]{:S(2)}) collective-permute-start(bf16[512,256]{1,0:T(8,128)(2,1)S(1)} %get-tuple-element.30), channel_id=1, source_target_pairs={{0,4},{4,8},{8,12},{12,16},{16,20},{20,24},{24,28},{28,0},{1,5},{5... | collective-permute-start | bytes 786440 | tf_op jit(solution)/shard_map/ppermute | solution.py:18
  72.0 10.8 %copy-start.1 = (f32[1,1,2,512,256]{4,3,2,1,0:T(8,128)S(1)}, f32[1,1,2,512,256]{4,3,2,1,0:T(8,128)}, u32[]{:S(2)}) copy-start(f32[1,1,2,512,256]{4,3,2,1,0:T(8,128)} %param.11) | copy-start | bytes 3145732
  72.0 10.6 %collective-permute-start.2 = (bf16[512,256]{1,0:T(8,128)(2,1)S(1)}, bf16[512,256]{1,0:T(8,128)(2,1)S(1)}, u32[]{:S(2)}, u32[]{:S(2)}) collective-permute-start(bf16[512,256]{1,0:T(8,128)(2,1)S(1)} %get-tuple-element.25), channel_id=1, source_target_pairs={{1,0},{2,1},{3,2},{5,4},{6,5},{7,6},{9,8},{10,9},{11,10},{13,12},{... | collective-permute-start | bytes 786440 | tf_op jit(solution)/shard_map/ppermute | solution.py:12
  73.5 9.2 %collective-permute-start.3 = (bf16[512,256]{1,0:T(8,128)(2,1)S(1)}, bf16[512,256]{1,0:T(8,128)(2,1)S(1)}, u32[]{:S(2)}, u32[]{:S(2)}) collective-permute-start(bf16[512,256]{1,0:T(8,128)(2,1)S(1)} %get-tuple-element.26), channel_id=1, source_target_pairs={{0,28},{4,0},{8,4},{12,8},{16,12},{20,16},{24,20},{28,24},{1,29},{... | collective-permute-start | bytes 786440 | tf_op jit(solution)/shard_map/ppermute | solution.py:18
  82.8 33.6 %copy-start.2 = (f32[1,1,1,512,256]{4,3,2,1,0:T(8,128)}, f32[1,1,1,512,256]{4,3,2,1,0:T(8,128)S(1)}, u32[]{:S(2)}) copy-start(f32[1,1,1,512,256]{4,3,2,1,0:T(8,128)S(1)} %get-tuple-element.13) | copy-start | bytes 1572868
  82.8 33.6 %copy-start.4 = (f32[1,1,1,512,256]{4,3,2,1,0:T(8,128)}, f32[1,1,1,512,256]{4,3,2,1,0:T(8,128)S(1)}, u32[]{:S(2)}) copy-start(f32[1,1,1,512,256]{4,3,2,1,0:T(8,128)S(1)} %get-tuple-element.22) | copy-start | bytes 1572868
  83.1 3.6 %collective-permute-start.4 = (f32[2,256]{1,0:T(2,128)S(1)}, f32[2,256]{1,0:T(2,128)S(1)}, u32[]{:S(2)}, u32[]{:S(2)}) collective-permute-start(f32[2,256]{1,0:T(2,128)S(1)} %pad_maximum_fusion.2), channel_id=1, source_target_pairs={{0,1},{1,0},{2,3},{3,2},{4,5},{5,4},{6,7},{7,6},{8,9},{9,8},{10,11... | collective-permute-start | bytes 6152 | tf_op jit(solution)/shard_map/ppermute | solution.py:29
  86.7 4.5 %collective-permute-start.5 = (f32[2,256]{1,0:T(2,128)S(1)}, f32[2,256]{1,0:T(2,128)S(1)}, u32[]{:S(2)}, u32[]{:S(2)}) collective-permute-start(f32[2,256]{1,0:T(2,128)S(1)} %fusion.42), channel_id=1, source_target_pairs={{0,2},{1,3},{2,0},{3,1},{4,6},{5,7},{6,4},{7,5},{8,10},{9,11},{10,... | collective-permute-start | bytes 6152 | tf_op jit(solution)/shard_map/ppermute | solution.py:29
  91.3 1.2 collective-permute-start.6
  92.5 3.6 %collective-permute-start.7 = (f32[2,256]{1,0:T(2,128)S(1)}, f32[2,256]{1,0:T(2,128)S(1)}, u32[]{:S(2)}, u32[]{:S(2)}) collective-permute-start(f32[2,256]{1,0:T(2,128)S(1)} %add.115), channel_id=1, source_target_pairs={{0,8},{4,12},{8,0},{12,4},{16,24},{20,28},{24,16},{28,20},{1,9},{5... | collective-permute-start | bytes 6152 | tf_op jit(solution)/shard_map/ppermute | solution.py:29
  96.1 3.6 %collective-permute-start.8 = (f32[2,256]{1,0:T(2,128)S(1)}, f32[2,256]{1,0:T(2,128)S(1)}, u32[]{:S(2)}, u32[]{:S(2)}) collective-permute-start(f32[2,256]{1,0:T(2,128)S(1)} %add.116), channel_id=1, source_target_pairs={{0,16},{4,20},{8,24},{12,28},{16,0},{20,4},{24,8},{28,12},{1,17},{... | collective-permute-start | bytes 6152 | tf_op jit(solution)/shard_map/ppermute | solution.py:29
  100.0 3.6 %collective-permute-start.9 = (f32[256]{0:T(256)S(1)}, f32[256]{0:T(256)S(1)}, u32[]{:S(2)}, u32[]{:S(2)}) collective-permute-start(f32[256]{0:T(256)S(1)} %multiply_reduce_fusion), channel_id=1, source_target_pairs={{0,1},{1,0},{2,3},{3,2},{4,5},{5,4},{6,7},{7,6},{8,9},{9,8},{10,11... | collective-permute-start | bytes 3080 | tf_op jit(solution)/shard_map/ppermute | solution.py:29
  103.6 4.5 %collective-permute-start.10 = (f32[256]{0:T(256)S(1)}, f32[256]{0:T(256)S(1)}, u32[]{:S(2)}, u32[]{:S(2)}) collective-permute-start(f32[256]{0:T(256)S(1)} %add.118), channel_id=1, source_target_pairs={{0,2},{1,3},{2,0},{3,1},{4,6},{5,7},{6,4},{7,5},{8,10},{9,11},{10,... | collective-permute-start | bytes 3080 | tf_op jit(solution)/shard_map/ppermute | solution.py:29
  108.1 1.2 collective-permute-start.11
  109.2 3.6 %collective-permute-start.12 = (f32[256]{0:T(256)S(1)}, f32[256]{0:T(256)S(1)}, u32[]{:S(2)}, u32[]{:S(2)}) collective-permute-start(f32[256]{0:T(256)S(1)} %add.120), channel_id=1, source_target_pairs={{0,8},{4,12},{8,0},{12,4},{16,24},{20,28},{24,16},{28,20},{1,9},{5... | collective-permute-start | bytes 3080 | tf_op jit(solution)/shard_map/ppermute | solution.py:29
  112.8 3.6 %collective-permute-start.13 = (f32[256]{0:T(256)S(1)}, f32[256]{0:T(256)S(1)}, u32[]{:S(2)}, u32[]{:S(2)}) collective-permute-start(f32[256]{0:T(256)S(1)} %add.121), channel_id=1, source_target_pairs={{0,16},{4,20},{8,24},{12,28},{16,0},{20,4},{24,8},{28,12},{1,17},{... | collective-permute-start | bytes 3080 | tf_op jit(solution)/shard_map/ppermute | solution.py:29
  116.6 5.8 %collective-permute-start.14 = (bf16[512,256]{1,0:T(8,128)(2,1)S(1)}, bf16[512,256]{1,0:T(8,128)(2,1)S(1)}, u32[]{:S(2)}, u32[]{:S(2)}) collective-permute-start(bf16[512,256]{1,0:T(8,128)(2,1)S(1)} %get-tuple-element.27), channel_id=1, source_target_pairs={{0,1},{1,2},{2,3},{4,5},{5,6},{6,7},{8,9},{9,10},{10,11},{12,13},{... | collective-permute-start | bytes 786440 | tf_op jit(solution)/shard_map/ppermute | solution.py:12
  118.6 6.7 %collective-permute-start.15 = (bf16[512,256]{1,0:T(8,128)(2,1)S(1)}, bf16[512,256]{1,0:T(8,128)(2,1)S(1)}, u32[]{:S(2)}, u32[]{:S(2)}) collective-permute-start(bf16[512,256]{1,0:T(8,128)(2,1)S(1)} %get-tuple-element.28), channel_id=1, source_target_pairs={{0,4},{4,8},{8,12},{12,16},{16,20},{20,24},{24,28},{28,0},{1,5},{5... | collective-permute-start | bytes 786440 | tf_op jit(solution)/shard_map/ppermute | solution.py:18
  181.0 10.8 %copy-start.3 = (f32[1,1,1,512,256]{4,3,2,1,0:T(8,128)S(1)}, f32[1,1,1,512,256]{4,3,2,1,0:T(8,128)}, u32[]{:S(2)}) copy-start(f32[1,1,1,512,256]{4,3,2,1,0:T(8,128)} %copy-done.2) | copy-start | bytes 1572868
  181.0 10.8 %copy-start.5 = (f32[1,1,1,512,256]{4,3,2,1,0:T(8,128)S(1)}, f32[1,1,1,512,256]{4,3,2,1,0:T(8,128)}, u32[]{:S(2)}) copy-start(f32[1,1,1,512,256]{4,3,2,1,0:T(8,128)} %copy-done.4) | copy-start | bytes 1572868
  181.0 10.6 %collective-permute-start.16 = (bf16[512,256]{1,0:T(8,128)(2,1)S(1)}, bf16[512,256]{1,0:T(8,128)(2,1)S(1)}, u32[]{:S(2)}, u32[]{:S(2)}) collective-permute-start(bf16[512,256]{1,0:T(8,128)(2,1)S(1)} %get-tuple-element.23), channel_id=1, source_target_pairs={{1,0},{2,1},{3,2},{5,4},{6,5},{7,6},{9,8},{10,9},{11,10},{13,12},{... | collective-permute-start | bytes 786440 | tf_op jit(solution)/shard_map/ppermute | solution.py:12
  182.4 9.2 %collective-permute-start.17 = (bf16[512,256]{1,0:T(8,128)(2,1)S(1)}, bf16[512,256]{1,0:T(8,128)(2,1)S(1)}, u32[]{:S(2)}, u32[]{:S(2)}) collective-permute-start(bf16[512,256]{1,0:T(8,128)(2,1)S(1)} %get-tuple-element.24), channel_id=1, source_target_pairs={{0,28},{4,0},{8,4},{12,8},{16,12},{20,16},{24,20},{28,24},{1,29},{... | collective-permute-start | bytes 786440 | tf_op jit(solution)/shard_map/ppermute | solution.py:18
  192.1 3.6 %collective-permute-start.18 = (f32[256]{0:T(256)S(1)}, f32[256]{0:T(256)S(1)}, u32[]{:S(2)}, u32[]{:S(2)}) collective-permute-start(f32[256]{0:T(256)S(1)} %fusion.14), channel_id=1, source_target_pairs={{0,1},{1,0},{2,3},{3,2},{4,5},{5,4},{6,7},{7,6},{8,9},{9,8},{10,11... | collective-permute-start | bytes 3080 | tf_op jit(solution)/shard_map/ppermute | solution.py:29
  195.7 4.5 %collective-permute-start.19 = (f32[256]{0:T(256)S(1)}, f32[256]{0:T(256)S(1)}, u32[]{:S(2)}, u32[]{:S(2)}) collective-permute-start(f32[256]{0:T(256)S(1)} %add.124), channel_id=1, source_target_pairs={{0,2},{1,3},{2,0},{3,1},{4,6},{5,7},{6,4},{7,5},{8,10},{9,11},{10,... | collective-permute-start | bytes 3080 | tf_op jit(solution)/shard_map/ppermute | solution.py:29
  200.2 1.2 collective-permute-start.20
  201.3 3.6 %collective-permute-start.21 = (f32[256]{0:T(256)S(1)}, f32[256]{0:T(256)S(1)}, u32[]{:S(2)}, u32[]{:S(2)}) collective-permute-start(f32[256]{0:T(256)S(1)} %add.126), channel_id=1, source_target_pairs={{0,8},{4,12},{8,0},{12,4},{16,24},{20,28},{24,16},{28,20},{1,9},{5... | collective-permute-start | bytes 3080 | tf_op jit(solution)/shard_map/ppermute | solution.py:29
  204.9 3.6 %collective-permute-start.22 = (f32[256]{0:T(256)S(1)}, f32[256]{0:T(256)S(1)}, u32[]{:S(2)}, u32[]{:S(2)}) collective-permute-start(f32[256]{0:T(256)S(1)} %add.127), channel_id=1, source_target_pairs={{0,16},{4,20},{8,24},{12,28},{16,0},{20,4},{24,8},{28,12},{1,17},{... | collective-permute-start | bytes 3080 | tf_op jit(solution)/shard_map/ppermute | solution.py:29

commit v3 on v2

--- a/solution.py
+++ b/solution.py
@@ -31,6 +31,13 @@
     return x
 
 
+def gathered(x, axis):
+    count = lax.axis_size(axis)
+    return [x] + [
+        lax.ppermute(x, axis, [(i, (i + k) % count) for i in range(count)]) for k in range(1, count)
+    ]
+
+
 def squares(residual):
     return total(jnp.sum(residual * residual, axis=(0, 1, 2, 3)))
 
@@ -49,6 +56,15 @@
     face_width = slot_order.shape[0] // 4
     cases = dual_load.shape[-1]
     sub_count = lax.axis_size("sub")
+    sub_id = lax.axis_index("sub")
+    sector_count = lax.axis_size("sector")
+    sector_id = lax.axis_index("sector")
+    inverse_rows = lax.dynamic_slice_in_dim(coarse_inverse, sector_id * corner_count, corner_count, 0)
+    inverse_by_shift = jnp.take(
+        inverse_rows.reshape(corner_count, sector_count, corner_count),
+        (sector_id - jnp.arange(sector_count)) % sector_count,
+        axis=1,
+    ).reshape(corner_count, sector_count * corner_count)
     multiplier = jnp.zeros_like(dual_load)
     residual = dual_load
     direction = dual_load
@@ -57,15 +73,15 @@
         lower_sub = passed_along(rounded[0], "sub", 1)
         previous = from_behind(rounded[1], "sector", 1)
         face_stack = jnp.concatenate([-lower_sub, rounded[0], -previous, rounded[1]], axis=0)
-        partial_value = jnp.take(face_stack, corners, axis=0).astype(jnp.float32)
-        sector_total = lax.psum(partial_value.astype(jnp.bfloat16), "sub").astype(jnp.float32)
-        sector_id = lax.axis_index("sector")
-        everything = lax.all_gather(sector_total, "sector", axis=0, tiled=True)
-        inverse_rows = lax.dynamic_slice_in_dim(
-            coarse_inverse, sector_id * corner_count, corner_count, 0
-        )
+        partial_value = jnp.take(face_stack, corners, axis=0)
+        pieces = jnp.stack(gathered(partial_value, "sub")).astype(jnp.float32)
+        pieces = jnp.take(pieces, (sub_id - jnp.arange(sub_count)) % sub_count, axis=0)
+        sector_total = pieces[0]
+        for k in range(1, sub_count):
+            sector_total = sector_total + pieces[k]
+        everything = jnp.concatenate(gathered(sector_total, "sector"), axis=0)
         coarse = jnp.dot(
-            inverse_rows,
+            inverse_by_shift,
             everything,
             precision=lax.Precision.HIGHEST,
             preferred_element_type=jnp.float32,

time: 211 us -> 201 us (0.953)
  blocking collectives: 51.9 us -> 0 us
  starting transfers between devices: 20.3 us -> 40.8 us
  waiting for transfers between devices: 63.9 us -> 80.3 us
  local copies, waits for them, and re-layouts: 45.5 us -> 48.5 us
    psum x2 -> x0, blocking collectives: 33.1 us -> none  [shards(): lax.psum(partial_value.astype(jnp.bfloat16), 'sub').astype(jnp.float32)]
    ppermute x0 -> x20, starting transfers between devices: none -> 22.9 us  [gathered(): lax.ppermute(x, axis, [(i, (i + k) % count) for i in range(count)])]
    all_gather x2 -> x0, blocking collectives: 18.8 us -> none  [shards(): everything = lax.all_gather(sector_total, 'sector', axis=0, tiled=True)]
    ppermute x0 -> x20, waiting for transfers between devices: none -> 13.1 us  [gathered(): lax.ppermute(x, axis, [(i, (i + k) % count) for i in range(count)])]
  transfers between devices with their start and end apart: 23 -> 43, of which waited for: 19 -> 23; matrix products, arithmetic and copies ran while one was open for 4% -> 29% of each run, Pallas kernels for 0% -> 0%
where the time goes in v3:
time: 201 us
  waiting for transfers between devices  80.3 us (40%)
  local copies, waits for them, and re-layouts  48.5 us (24%)
  starting transfers between devices  40.8 us (20%)
  matrix products  15.5 us (8%)
  other arithmetic  14.1 us (7%)
    ppermute x15, waiting for transfers between devices, total(): x = x + lax.ppermute(x, axis, [(i, i ^ step) for i in range(count)])  43.4 us
    ppermute x20, starting transfers between devices, gathered(): lax.ppermute(x, axis, [(i, (i + k) % count) for i in range(count)])  22.9 us
    ppermute x4, waiting for transfers between devices, passed_along(): return lax.ppermute(x, axis, pairs)  21 us
    gather x2, local copies, waits for them, and re-layouts, shards(): product = jnp.take(own_product, slot_order, axis=0) + correction  17.2 us
    dot_general x2, matrix products, shards(): own_product = jnp.dot(matrix, own_faces, preferred_element_type=jnp.float32)  15 us
    gather x2, local copies, waits for them, and re-layouts, shards(): own_faces = jnp.take(face_stack, own_place, axis=0)  15 us
    ppermute x20, waiting for transfers between devices, gathered(): lax.ppermute(x, axis, [(i, (i + k) % count) for i in range(count)])  13.1 us
    ppermute x4, starting transfers between devices, passed_along(): return lax.ppermute(x, axis, pairs)  9.75 us
  transfers between devices with their start and end apart: 43, of which 23 were waited for; matrix products, arithmetic and copies ran while one was open for 29% of the time, Pallas kernels for 0%

profile of v3, /device:TPU:0, one launch (start us, length us, event | category | flops | bytes accessed | tf_op | source)
XLA Modules:
  0.0 200.9 jit_solution(7667953258966030684)
XLA Ops:
  2.0 5.0 %collective-permute-start = (bf16[512,256]{1,0:T(8,128)(2,1)S(1)}, bf16[512,256]{1,0:T(8,128)(2,1)S(1)}, u32[]{:S(2)}, u32[]{:S(2)}) collective-permute-start(bf16[512,256]{1,0:T(8,128)(2,1)S(1)} %get-tuple-element.34), channel_id=1, source_target_pairs={{0,1},{1,2},{2,3},{4,5},{5,6},{6,7},{8,9},{9,10},{10,11},{12,13},{... | collective-permute-start | bytes 786440 | tf_op jit(solution)/shard_map/ppermute | solution.py:12
  8.4 8.0 %scatter_custom_fusion = s32[2048]{0:T(1024)S(1)} fusion(s32[2048]{0:T(1024)S(1)} %bitcast.104, s32[2048]{0:T(1024)S(1)} %iota.13, s32[]{:T(128)} %constant.79.clone.1), kind=kCustom, calls=%fused_computation.107 | custom fusion | bytes 8196 | tf_op jit(solution)/shard_map/scatter | solution.py:54
  19.0 2.6 %collective-permute-start.3 = (bf16[32,256]{1,0:T(8,128)(2,1)S(1)}, bf16[32,256]{1,0:T(8,128)(2,1)S(1)}, u32[]{:S(2)}, u32[]{:S(2)}) collective-permute-start(bf16[32,256]{1,0:T(8,128)(2,1)S(1)} %broadcast_select_fusion.5), channel_id=1, source_target_pairs={{0,2},{1,3},{2,0},{3,1},{4,6},{5,7},{6,4},{7,5},{8,10},{9,11},{10,... | collective-permute-start | bytes 49160 | tf_op jit(solution)/shard_map/ppermute | solution.py:37
  21.6 3.8 %collective-permute-start.4 = (bf16[32,256]{1,0:T(8,128)(2,1)S(1)}, bf16[32,256]{1,0:T(8,128)(2,1)S(1)}, u32[]{:S(2)}, u32[]{:S(2)}) collective-permute-start(bf16[32,256]{1,0:T(8,128)(2,1)S(1)} %broadcast_select_fusion.5), channel_id=1, source_target_pairs={{0,3},{1,0},{2,1},{3,2},{4,7},{5,4},{6,5},{7,6},{8,11},{9,8},{10,9... | collective-permute-start | bytes 49160 | tf_op jit(solution)/shard_map/ppermute | solution.py:37
  25.4 7.5 %gather_fusion.1 = bf16[2048,256]{1,0:T(8,128)(2,1)S(1)} fusion(bf16[2048,256]{1,0:T(8,128)(2,1)S(1)} %pad_maximum_fusion, s32[2048]{0:T(1024)S(1)} %fusion.39), kind=kCustom, calls=%fused_computation.clone | custom fusion | bytes 2105344 | tf_op jit(solution)/shard_map/jit(_take)/gather | solution.py:91
  33.0 7.5 %fusion.4 = f32[2048,256]{0,1:T(8,128)} fusion(bf16[1,1,2048,2048]{3,2,1,0:T(8,128)(2,1)} %param.14, bf16[2048,256]{1,0:T(8,128)(2,1)S(1)} %gather_fusion.1, pred[2048]{0:T(1024)(128)(4,1)S(1)} %compare_and_fusion.1), kind=kOutput, calls=%fused_computation.16 | convolution fusion | flops 2148007936 | bytes 11536384 | tf_op jit(solution)/shard_map/dot_general | solution.py:92
  42.5 8.6 %gather_fusion.2 = f32[2048,256]{1,0:T(8,128)} fusion(f32[2048,256]{1,0:T(8,128)S(1)} %copy.11, s32[2048]{0:T(1024)S(1)} %fusion.40), kind=kCustom, calls=%fused_computation.1.clone | custom fusion | bytes 4202496 | tf_op jit(solution)/shard_map/jit(_take)/gather | solution.py:93
  60.0 3.4 %collective-permute-done.6 = f32[32,256]{1,0:T(8,128)S(1)} collective-permute-done((f32[32,256]{1,0:T(8,128)S(1)}, f32[32,256]{1,0:T(8,128)S(1)}, u32[]{:S(2)}, u32[]{:S(2)}) %collective-permute-start.6) | collective-permute-done | bytes 32800 | tf_op jit(solution)/shard_map/ppermute | solution.py:37
  63.4 3.3 %collective-permute-done.7 = f32[32,256]{1,0:T(8,128)S(1)} collective-permute-done((f32[32,256]{1,0:T(8,128)S(1)}, f32[32,256]{1,0:T(8,128)S(1)}, u32[]{:S(2)}, u32[]{:S(2)}) %collective-permute-start.7) | collective-permute-done | bytes 32800 | tf_op jit(solution)/shard_map/ppermute | solution.py:37
  71.3 8.7 %collective-permute-done.12 = bf16[512,256]{1,0:T(8,128)(2,1)S(1)} collective-permute-done((bf16[512,256]{1,0:T(8,128)(2,1)S(1)}, bf16[512,256]{1,0:T(8,128)(2,1)S(1)}, u32[]{:S(2)}, u32[]{:S(2)}) %collective-permute-start.12) | collective-permute-done | bytes 262176 | tf_op jit(solution)/shard_map/ppermute | solution.py:12
  80.5 3.6 %collective-permute-done.14 = f32[2,256]{1,0:T(2,128)S(1)} collective-permute-done((f32[2,256]{1,0:T(2,128)S(1)}, f32[2,256]{1,0:T(2,128)S(1)}, u32[]{:S(2)}, u32[]{:S(2)}) %collective-permute-start.14) | collective-permute-done | bytes 2080 | tf_op jit(solution)/shard_map/ppermute | solution.py:29
  84.2 4.5 %collective-permute-done.15 = f32[2,256]{1,0:T(2,128)S(1)} collective-permute-done((f32[2,256]{1,0:T(2,128)S(1)}, f32[2,256]{1,0:T(2,128)S(1)}, u32[]{:S(2)}, u32[]{:S(2)}) %collective-permute-start.15) | collective-permute-done | bytes 2080 | tf_op jit(solution)/shard_map/ppermute | solution.py:29
  89.9 3.6 %collective-permute-done.17 = f32[2,256]{1,0:T(2,128)S(1)} collective-permute-done((f32[2,256]{1,0:T(2,128)S(1)}, f32[2,256]{1,0:T(2,128)S(1)}, u32[]{:S(2)}, u32[]{:S(2)}) %collective-permute-start.17) | collective-permute-done | bytes 2080 | tf_op jit(solution)/shard_map/ppermute | solution.py:29
  95.0 2.1 %collective-permute-done.18 = f32[2,256]{1,0:T(2,128)S(1)} collective-permute-done((f32[2,256]{1,0:T(2,128)S(1)}, f32[2,256]{1,0:T(2,128)S(1)}, u32[]{:S(2)}, u32[]{:S(2)}) %collective-permute-start.18) | collective-permute-done | bytes 2080 | tf_op jit(solution)/shard_map/ppermute | solution.py:29
  97.4 3.6 %collective-permute-done.19 = f32[256]{0:T(256)S(1)} collective-permute-done((f32[256]{0:T(256)S(1)}, f32[256]{0:T(256)S(1)}, u32[]{:S(2)}, u32[]{:S(2)}) %collective-permute-start.19) | collective-permute-done | bytes 1056 | tf_op jit(solution)/shard_map/ppermute | solution.py:29
  100.9 4.5 %collective-permute-done.20 = f32[256]{0:T(256)S(1)} collective-permute-done((f32[256]{0:T(256)S(1)}, f32[256]{0:T(256)S(1)}, u32[]{:S(2)}, u32[]{:S(2)}) %collective-permute-start.20) | collective-permute-done | bytes 1056 | tf_op jit(solution)/shard_map/ppermute | solution.py:29
  106.6 3.6 %collective-permute-done.22 = f32[256]{0:T(256)S(1)} collective-permute-done((f32[256]{0:T(256)S(1)}, f32[256]{0:T(256)S(1)}, u32[]{:S(2)}, u32[]{:S(2)}) %collective-permute-start.22) | collective-permute-done | bytes 1056 | tf_op jit(solution)/shard_map/ppermute | solution.py:29
  111.7 2.1 %collective-permute-done.23 = f32[256]{0:T(256)S(1)} collective-permute-done((f32[256]{0:T(256)S(1)}, f32[256]{0:T(256)S(1)}, u32[]{:S(2)}, u32[]{:S(2)}) %collective-permute-start.23) | collective-permute-done | bytes 1056 | tf_op jit(solution)/shard_map/ppermute | solution.py:29
  116.6 3.8 %collective-permute-done.24 = bf16[512,256]{1,0:T(8,128)(2,1)S(1)} collective-permute-done((bf16[512,256]{1,0:T(8,128)(2,1)S(1)}, bf16[512,256]{1,0:T(8,128)(2,1)S(1)}, u32[]{:S(2)}, u32[]{:S(2)}) %collective-permute-start.24) | collective-permute-done | bytes 262176 | tf_op jit(solution)/shard_map/ppermute | solution.py:12
  120.4 2.8 %collective-permute-done.25 = bf16[512,256]{1,0:T(8,128)(2,1)S(1)} collective-permute-done((bf16[512,256]{1,0:T(8,128)(2,1)S(1)}, bf16[512,256]{1,0:T(8,128)(2,1)S(1)}, u32[]{:S(2)}, u32[]{:S(2)}) %collective-permute-start.25) | collective-permute-done | bytes 262176 | tf_op jit(solution)/shard_map/ppermute | solution.py:18
  124.1 7.5 %gather_fusion.5 = bf16[2048,256]{1,0:T(8,128)(2,1)S(1)} fusion(bf16[2048,256]{1,0:T(8,128)(2,1)S(1)} %pad_maximum_fusion.1, s32[2048]{0:T(1024)S(1)} %fusion.39), kind=kCustom, calls=%fused_computation.4.clone | custom fusion | bytes 2105344 | tf_op jit(solution)/shard_map/jit(_take)/gather | solution.py:91
  132.4 3.3 %collective-permute-start.28 = (bf16[32,256]{1,0:T(8,128)(2,1)S(1)}, bf16[32,256]{1,0:T(8,128)(2,1)S(1)}, u32[]{:S(2)}, u32[]{:S(2)}) collective-permute-start(bf16[32,256]{1,0:T(8,128)(2,1)S(1)} %broadcast_select_fusion.4), channel_id=1, source_target_pairs={{0,3},{1,0},{2,1},{3,2},{4,7},{5,4},{6,5},{7,6},{8,11},{9,8},{10,9... | collective-permute-start | bytes 49160 | tf_op jit(solution)/shard_map/ppermute | solution.py:37
  135.6 7.5 %fusion.7 = f32[2048,256]{0,1:T(8,128)} fusion(bf16[1,1,2048,2048]{3,2,1,0:T(8,128)(2,1)} %param.14, bf16[2048,256]{1,0:T(8,128)(2,1)S(1)} %gather_fusion.5, pred[2048]{0:T(1024)(128)(4,1)S(1)} %copy-done.22), kind=kOutput, calls=%fused_computation.17 | convolution fusion | flops 2148007936 | bytes 11536384 | tf_op jit(solution)/shard_map/dot_general | solution.py:92
  145.2 8.6 %gather_fusion.6 = f32[2048,256]{1,0:T(8,128)} fusion(f32[2048,256]{1,0:T(8,128)S(1)} %copy.14, s32[2048]{0:T(1024)S(1)} %fusion.40), kind=kCustom, calls=%fused_computation.5.clone | custom fusion | bytes 4202496 | tf_op jit(solution)/shard_map/jit(_take)/gather | solution.py:93
  156.6 2.7 %collective-permute-start.35 = (f32[32,256]{1,0:T(8,128)S(1)}, f32[32,256]{1,0:T(8,128)S(1)}, u32[]{:S(2)}, u32[]{:S(2)}) collective-permute-start(f32[32,256]{1,0:T(8,128)S(1)} %get-tuple-element.9), channel_id=1, source_target_pairs={{0,28},{4,0},{8,4},{12,8},{16,12},{20,16},{24,20},{28,24},{1,29},{... | collective-permute-start | bytes 98312 | tf_op jit(solution)/shard_map/ppermute | solution.py:37
  162.8 3.1 %collective-permute-done.30 = f32[32,256]{1,0:T(8,128)S(1)} collective-permute-done((f32[32,256]{1,0:T(8,128)S(1)}, f32[32,256]{1,0:T(8,128)S(1)}, u32[]{:S(2)}, u32[]{:S(2)}) %collective-permute-start.30) | collective-permute-done | bytes 32800 | tf_op jit(solution)/shard_map/ppermute | solution.py:37
  166.0 3.3 %collective-permute-done.31 = f32[32,256]{1,0:T(8,128)S(1)} collective-permute-done((f32[32,256]{1,0:T(8,128)S(1)}, f32[32,256]{1,0:T(8,128)S(1)}, u32[]{:S(2)}, u32[]{:S(2)}) %collective-permute-start.31) | collective-permute-done | bytes 32800 | tf_op jit(solution)/shard_map/ppermute | solution.py:37
  173.8 8.5 %collective-permute-done.36 = bf16[512,256]{1,0:T(8,128)(2,1)S(1)} collective-permute-done((bf16[512,256]{1,0:T(8,128)(2,1)S(1)}, bf16[512,256]{1,0:T(8,128)(2,1)S(1)}, u32[]{:S(2)}, u32[]{:S(2)}) %collective-permute-start.36) | collective-permute-done | bytes 262176 | tf_op jit(solution)/shard_map/ppermute | solution.py:12
  182.8 3.6 %collective-permute-done.38 = f32[256]{0:T(256)S(1)} collective-permute-done((f32[256]{0:T(256)S(1)}, f32[256]{0:T(256)S(1)}, u32[]{:S(2)}, u32[]{:S(2)}) %collective-permute-start.38) | collective-permute-done | bytes 1056 | tf_op jit(solution)/shard_map/ppermute | solution.py:29
  187.5 3.4 %collective-permute-done.39 = f32[256]{0:T(256)S(1)} collective-permute-done((f32[256]{0:T(256)S(1)}, f32[256]{0:T(256)S(1)}, u32[]{:S(2)}, u32[]{:S(2)}) %collective-permute-start.39) | collective-permute-done | bytes 1056 | tf_op jit(solution)/shard_map/ppermute | solution.py:29
  192.1 3.5 %collective-permute-done.41 = f32[256]{0:T(256)S(1)} collective-permute-done((f32[256]{0:T(256)S(1)}, f32[256]{0:T(256)S(1)}, u32[]{:S(2)}, u32[]{:S(2)}) %collective-permute-start.41) | collective-permute-done | bytes 1056 | tf_op jit(solution)/shard_map/ppermute | solution.py:29
  197.1 2.1 %collective-permute-done.42 = f32[256]{0:T(256)S(1)} collective-permute-done((f32[256]{0:T(256)S(1)}, f32[256]{0:T(256)S(1)}, u32[]{:S(2)}, u32[]{:S(2)}) %collective-permute-start.42) | collective-permute-done | bytes 1056 | tf_op jit(solution)/shard_map/ppermute | solution.py:29
  (207 shorter events, 49.9 us)
Async XLA Ops:
  2.0 16.1 %collective-permute-start = (bf16[512,256]{1,0:T(8,128)(2,1)S(1)}, bf16[512,256]{1,0:T(8,128)(2,1)S(1)}, u32[]{:S(2)}, u32[]{:S(2)}) collective-permute-start(bf16[512,256]{1,0:T(8,128)(2,1)S(1)} %get-tuple-element.34), channel_id=1, source_target_pairs={{0,1},{1,2},{2,3},{4,5},{5,6},{6,7},{8,9},{9,10},{10,11},{12,13},{... | collective-permute-start | bytes 786440 | tf_op jit(solution)/shard_map/ppermute | solution.py:12
  7.0 11.2 %collective-permute-start.1 = (bf16[512,256]{1,0:T(8,128)(2,1)S(1)}, bf16[512,256]{1,0:T(8,128)(2,1)S(1)}, u32[]{:S(2)}, u32[]{:S(2)}) collective-permute-start(bf16[512,256]{1,0:T(8,128)(2,1)S(1)} %get-tuple-element.35), channel_id=1, source_target_pairs={{0,4},{4,8},{8,12},{12,16},{16,20},{20,24},{24,28},{28,0},{1,5},{5... | collective-permute-start | bytes 786440 | tf_op jit(solution)/shard_map/ppermute | solution.py:18
  19.0 32.0 %collective-permute-start.3 = (bf16[32,256]{1,0:T(8,128)(2,1)S(1)}, bf16[32,256]{1,0:T(8,128)(2,1)S(1)}, u32[]{:S(2)}, u32[]{:S(2)}) collective-permute-start(bf16[32,256]{1,0:T(8,128)(2,1)S(1)} %broadcast_select_fusion.5), channel_id=1, source_target_pairs={{0,2},{1,3},{2,0},{3,1},{4,6},{5,7},{6,4},{7,5},{8,10},{9,11},{10,... | collective-permute-start | bytes 49160 | tf_op jit(solution)/shard_map/ppermute | solution.py:37
  21.6 29.4 %collective-permute-start.2 = (bf16[32,256]{1,0:T(8,128)(2,1)S(1)}, bf16[32,256]{1,0:T(8,128)(2,1)S(1)}, u32[]{:S(2)}, u32[]{:S(2)}) collective-permute-start(bf16[32,256]{1,0:T(8,128)(2,1)S(1)} %broadcast_select_fusion.5), channel_id=1, source_target_pairs={{0,1},{1,2},{2,3},{3,0},{4,5},{5,6},{6,7},{7,4},{8,9},{9,10},{10,1... | collective-permute-start | bytes 49160 | tf_op jit(solution)/shard_map/ppermute | solution.py:37
  21.6 29.4 %collective-permute-start.4 = (bf16[32,256]{1,0:T(8,128)(2,1)S(1)}, bf16[32,256]{1,0:T(8,128)(2,1)S(1)}, u32[]{:S(2)}, u32[]{:S(2)}) collective-permute-start(bf16[32,256]{1,0:T(8,128)(2,1)S(1)} %broadcast_select_fusion.5), channel_id=1, source_target_pairs={{0,3},{1,0},{2,1},{3,2},{4,7},{5,4},{6,5},{7,6},{8,11},{9,8},{10,9... | collective-permute-start | bytes 49160 | tf_op jit(solution)/shard_map/ppermute | solution.py:37
  51.8 6.7 %collective-permute-start.5 = (f32[32,256]{1,0:T(8,128)S(1)}, f32[32,256]{1,0:T(8,128)S(1)}, u32[]{:S(2)}, u32[]{:S(2)}) collective-permute-start(f32[32,256]{1,0:T(8,128)S(1)} %get-tuple-element.13), channel_id=1, source_target_pairs={{0,4},{4,8},{8,12},{12,16},{16,20},{20,24},{24,28},{28,0},{1,5},{5... | collective-permute-start | bytes 98312 | tf_op jit(solution)/shard_map/ppermute | solution.py:37
  54.5 12.3 %collective-permute-start.11 = (f32[32,256]{1,0:T(8,128)S(1)}, f32[32,256]{1,0:T(8,128)S(1)}, u32[]{:S(2)}, u32[]{:S(2)}) collective-permute-start(f32[32,256]{1,0:T(8,128)S(1)} %get-tuple-element.13), channel_id=1, source_target_pairs={{0,28},{4,0},{8,4},{12,8},{16,12},{20,16},{24,20},{28,24},{1,29},{... | collective-permute-start | bytes 98312 | tf_op jit(solution)/shard_map/ppermute | solution.py:37
  56.5 10.3 %collective-permute-start.10 = (f32[32,256]{1,0:T(8,128)S(1)}, f32[32,256]{1,0:T(8,128)S(1)}, u32[]{:S(2)}, u32[]{:S(2)}) collective-permute-start(f32[32,256]{1,0:T(8,128)S(1)} %get-tuple-element.13), channel_id=1, source_target_pairs={{0,24},{4,28},{8,0},{12,4},{16,8},{20,12},{24,16},{28,20},{1,25},{... | collective-permute-start | bytes 98312 | tf_op jit(solution)/shard_map/ppermute | solution.py:37
  58.0 8.7 %collective-permute-start.9 = (f32[32,256]{1,0:T(8,128)S(1)}, f32[32,256]{1,0:T(8,128)S(1)}, u32[]{:S(2)}, u32[]{:S(2)}) collective-permute-start(f32[32,256]{1,0:T(8,128)S(1)} %get-tuple-element.13), channel_id=1, source_target_pairs={{0,20},{4,24},{8,28},{12,0},{16,4},{20,8},{24,12},{28,16},{1,21},{... | collective-permute-start | bytes 98312 | tf_op jit(solution)/shard_map/ppermute | solution.py:37
  58.0 8.7 %collective-permute-start.8 = (f32[32,256]{1,0:T(8,128)S(1)}, f32[32,256]{1,0:T(8,128)S(1)}, u32[]{:S(2)}, u32[]{:S(2)}) collective-permute-start(f32[32,256]{1,0:T(8,128)S(1)} %get-tuple-element.13), channel_id=1, source_target_pairs={{0,16},{4,20},{8,24},{12,28},{16,0},{20,4},{24,8},{28,12},{1,17},{... | collective-permute-start | bytes 98312 | tf_op jit(solution)/shard_map/ppermute | solution.py:37
  58.6 4.9 %collective-permute-start.6 = (f32[32,256]{1,0:T(8,128)S(1)}, f32[32,256]{1,0:T(8,128)S(1)}, u32[]{:S(2)}, u32[]{:S(2)}) collective-permute-start(f32[32,256]{1,0:T(8,128)S(1)} %get-tuple-element.13), channel_id=1, source_target_pairs={{0,8},{4,12},{8,16},{12,20},{16,24},{20,28},{24,0},{28,4},{1,9},{5... | collective-permute-start | bytes 98312 | tf_op jit(solution)/shard_map/ppermute | solution.py:37
  68.8 11.2 %collective-permute-start.12 = (bf16[512,256]{1,0:T(8,128)(2,1)S(1)}, bf16[512,256]{1,0:T(8,128)(2,1)S(1)}, u32[]{:S(2)}, u32[]{:S(2)}) collective-permute-start(bf16[512,256]{1,0:T(8,128)(2,1)S(1)} %get-tuple-element.30), channel_id=1, source_target_pairs={{1,0},{2,1},{3,2},{5,4},{6,5},{7,6},{9,8},{10,9},{11,10},{13,12},{... | collective-permute-start | bytes 786440 | tf_op jit(solution)/shard_map/ppermute | solution.py:12
  70.3 9.7 %collective-permute-start.13 = (bf16[512,256]{1,0:T(8,128)(2,1)S(1)}, bf16[512,256]{1,0:T(8,128)(2,1)S(1)}, u32[]{:S(2)}, u32[]{:S(2)}) collective-permute-start(bf16[512,256]{1,0:T(8,128)(2,1)S(1)} %get-tuple-element.31), channel_id=1, source_target_pairs={{0,28},{4,0},{8,4},{12,8},{16,12},{20,16},{24,20},{28,24},{1,29},{... | collective-permute-start | bytes 786440 | tf_op jit(solution)/shard_map/ppermute | solution.py:18
  80.4 3.6 %collective-permute-start.14 = (f32[2,256]{1,0:T(2,128)S(1)}, f32[2,256]{1,0:T(2,128)S(1)}, u32[]{:S(2)}, u32[]{:S(2)}) collective-permute-start(f32[2,256]{1,0:T(2,128)S(1)} %pad_maximum_fusion.2), channel_id=1, source_target_pairs={{0,1},{1,0},{2,3},{3,2},{4,5},{5,4},{6,7},{7,6},{8,9},{9,8},{10,11... | collective-permute-start | bytes 6152 | tf_op jit(solution)/shard_map/ppermute | solution.py:29
  84.1 4.5 %collective-permute-start.15 = (f32[2,256]{1,0:T(2,128)S(1)}, f32[2,256]{1,0:T(2,128)S(1)}, u32[]{:S(2)}, u32[]{:S(2)}) collective-permute-start(f32[2,256]{1,0:T(2,128)S(1)} %fusion.52), channel_id=1, source_target_pairs={{0,2},{1,3},{2,0},{3,1},{4,6},{5,7},{6,4},{7,5},{8,10},{9,11},{10,... | collective-permute-start | bytes 6152 | tf_op jit(solution)/shard_map/ppermute | solution.py:29
  97.3 3.6 %collective-permute-start.19 = (f32[256]{0:T(256)S(1)}, f32[256]{0:T(256)S(1)}, u32[]{:S(2)}, u32[]{:S(2)}) collective-permute-start(f32[256]{0:T(256)S(1)} %multiply_reduce_fusion), channel_id=1, source_target_pairs={{0,1},{1,0},{2,3},{3,2},{4,5},{5,4},{6,7},{7,6},{8,9},{9,8},{10,11... | collective-permute-start | bytes 3080 | tf_op jit(solution)/shard_map/ppermute | solution.py:29
  100.9 4.5 %collective-permute-start.20 = (f32[256]{0:T(256)S(1)}, f32[256]{0:T(256)S(1)}, u32[]{:S(2)}, u32[]{:S(2)}) collective-permute-start(f32[256]{0:T(256)S(1)} %add.193), channel_id=1, source_target_pairs={{0,2},{1,3},{2,0},{3,1},{4,6},{5,7},{6,4},{7,5},{8,10},{9,11},{10,... | collective-permute-start | bytes 3080 | tf_op jit(solution)/shard_map/ppermute | solution.py:29
  114.6 5.8 %collective-permute-start.24 = (bf16[512,256]{1,0:T(8,128)(2,1)S(1)}, bf16[512,256]{1,0:T(8,128)(2,1)S(1)}, u32[]{:S(2)}, u32[]{:S(2)}) collective-permute-start(bf16[512,256]{1,0:T(8,128)(2,1)S(1)} %get-tuple-element.32), channel_id=1, source_target_pairs={{0,1},{1,2},{2,3},{4,5},{5,6},{6,7},{8,9},{9,10},{10,11},{12,13},{... | collective-permute-start | bytes 786440 | tf_op jit(solution)/shard_map/ppermute | solution.py:12
  116.5 6.7 %collective-permute-start.25 = (bf16[512,256]{1,0:T(8,128)(2,1)S(1)}, bf16[512,256]{1,0:T(8,128)(2,1)S(1)}, u32[]{:S(2)}, u32[]{:S(2)}) collective-permute-start(bf16[512,256]{1,0:T(8,128)(2,1)S(1)} %get-tuple-element.33), channel_id=1, source_target_pairs={{0,4},{4,8},{8,12},{12,16},{16,20},{20,24},{24,28},{28,0},{1,5},{5... | collective-permute-start | bytes 786440 | tf_op jit(solution)/shard_map/ppermute | solution.py:18
  131.7 22.0 %collective-permute-start.27 = (bf16[32,256]{1,0:T(8,128)(2,1)S(1)}, bf16[32,256]{1,0:T(8,128)(2,1)S(1)}, u32[]{:S(2)}, u32[]{:S(2)}) collective-permute-start(bf16[32,256]{1,0:T(8,128)(2,1)S(1)} %broadcast_select_fusion.4), channel_id=1, source_target_pairs={{0,2},{1,3},{2,0},{3,1},{4,6},{5,7},{6,4},{7,5},{8,10},{9,11},{10,... | collective-permute-start | bytes 49160 | tf_op jit(solution)/shard_map/ppermute | solution.py:37
  131.8 22.0 %collective-permute-start.26 = (bf16[32,256]{1,0:T(8,128)(2,1)S(1)}, bf16[32,256]{1,0:T(8,128)(2,1)S(1)}, u32[]{:S(2)}, u32[]{:S(2)}) collective-permute-start(bf16[32,256]{1,0:T(8,128)(2,1)S(1)} %broadcast_select_fusion.4), channel_id=1, source_target_pairs={{0,1},{1,2},{2,3},{3,0},{4,5},{5,6},{6,7},{7,4},{8,9},{9,10},{10,1... | collective-permute-start | bytes 49160 | tf_op jit(solution)/shard_map/ppermute | solution.py:37
  132.4 21.4 %collective-permute-start.28 = (bf16[32,256]{1,0:T(8,128)(2,1)S(1)}, bf16[32,256]{1,0:T(8,128)(2,1)S(1)}, u32[]{:S(2)}, u32[]{:S(2)}) collective-permute-start(bf16[32,256]{1,0:T(8,128)(2,1)S(1)} %broadcast_select_fusion.4), channel_id=1, source_target_pairs={{0,3},{1,0},{2,1},{3,2},{4,7},{5,4},{6,5},{7,6},{8,11},{9,8},{10,9... | collective-permute-start | bytes 49160 | tf_op jit(solution)/shard_map/ppermute | solution.py:37
  154.6 6.5 %collective-permute-start.29 = (f32[32,256]{1,0:T(8,128)S(1)}, f32[32,256]{1,0:T(8,128)S(1)}, u32[]{:S(2)}, u32[]{:S(2)}) collective-permute-start(f32[32,256]{1,0:T(8,128)S(1)} %get-tuple-element.9), channel_id=1, source_target_pairs={{0,4},{4,8},{8,12},{12,16},{16,20},{20,24},{24,28},{28,0},{1,5},{5... | collective-permute-start | bytes 98312 | tf_op jit(solution)/shard_map/ppermute | solution.py:37
  156.6 12.7 %collective-permute-start.35 = (f32[32,256]{1,0:T(8,128)S(1)}, f32[32,256]{1,0:T(8,128)S(1)}, u32[]{:S(2)}, u32[]{:S(2)}) collective-permute-start(f32[32,256]{1,0:T(8,128)S(1)} %get-tuple-element.9), channel_id=1, source_target_pairs={{0,28},{4,0},{8,4},{12,8},{16,12},{20,16},{24,20},{28,24},{1,29},{... | collective-permute-start | bytes 98312 | tf_op jit(solution)/shard_map/ppermute | solution.py:37
  159.3 10.0 %collective-permute-start.34 = (f32[32,256]{1,0:T(8,128)S(1)}, f32[32,256]{1,0:T(8,128)S(1)}, u32[]{:S(2)}, u32[]{:S(2)}) collective-permute-start(f32[32,256]{1,0:T(8,128)S(1)} %get-tuple-element.9), channel_id=1, source_target_pairs={{0,24},{4,28},{8,0},{12,4},{16,8},{20,12},{24,16},{28,20},{1,25},{... | collective-permute-start | bytes 98312 | tf_op jit(solution)/shard_map/ppermute | solution.py:37
  159.3 10.0 %collective-permute-start.33 = (f32[32,256]{1,0:T(8,128)S(1)}, f32[32,256]{1,0:T(8,128)S(1)}, u32[]{:S(2)}, u32[]{:S(2)}) collective-permute-start(f32[32,256]{1,0:T(8,128)S(1)} %get-tuple-element.9), channel_id=1, source_target_pairs={{0,20},{4,24},{8,28},{12,0},{16,4},{20,8},{24,12},{28,16},{1,21},{... | collective-permute-start | bytes 98312 | tf_op jit(solution)/shard_map/ppermute | solution.py:37
  160.6 8.7 %collective-permute-start.32 = (f32[32,256]{1,0:T(8,128)S(1)}, f32[32,256]{1,0:T(8,128)S(1)}, u32[]{:S(2)}, u32[]{:S(2)}) collective-permute-start(f32[32,256]{1,0:T(8,128)S(1)} %get-tuple-element.9), channel_id=1, source_target_pairs={{0,16},{4,20},{8,24},{12,28},{16,0},{20,4},{24,8},{28,12},{1,17},{... | collective-permute-start | bytes 98312 | tf_op jit(solution)/shard_map/ppermute | solution.py:37
  161.1 4.8 %collective-permute-start.30 = (f32[32,256]{1,0:T(8,128)S(1)}, f32[32,256]{1,0:T(8,128)S(1)}, u32[]{:S(2)}, u32[]{:S(2)}) collective-permute-start(f32[32,256]{1,0:T(8,128)S(1)} %get-tuple-element.9), channel_id=1, source_target_pairs={{0,8},{4,12},{8,16},{12,20},{16,24},{20,28},{24,0},{28,4},{1,9},{5... | collective-permute-start | bytes 98312 | tf_op jit(solution)/shard_map/ppermute | solution.py:37
  171.3 10.9 %collective-permute-start.36 = (bf16[512,256]{1,0:T(8,128)(2,1)S(1)}, bf16[512,256]{1,0:T(8,128)(2,1)S(1)}, u32[]{:S(2)}, u32[]{:S(2)}) collective-permute-start(bf16[512,256]{1,0:T(8,128)(2,1)S(1)} %get-tuple-element.28), channel_id=1, source_target_pairs={{1,0},{2,1},{3,2},{5,4},{6,5},{7,6},{9,8},{10,9},{11,10},{13,12},{... | collective-permute-start | bytes 786440 | tf_op jit(solution)/shard_map/ppermute | solution.py:12
  172.8 9.5 %collective-permute-start.37 = (bf16[512,256]{1,0:T(8,128)(2,1)S(1)}, bf16[512,256]{1,0:T(8,128)(2,1)S(1)}, u32[]{:S(2)}, u32[]{:S(2)}) collective-permute-start(bf16[512,256]{1,0:T(8,128)(2,1)S(1)} %get-tuple-element.29), channel_id=1, source_target_pairs={{0,28},{4,0},{8,4},{12,8},{16,12},{20,16},{24,20},{28,24},{1,29},{... | collective-permute-start | bytes 786440 | tf_op jit(solution)/shard_map/ppermute | solution.py:18
  182.8 3.6 %collective-permute-start.38 = (f32[256]{0:T(256)S(1)}, f32[256]{0:T(256)S(1)}, u32[]{:S(2)}, u32[]{:S(2)}) collective-permute-start(f32[256]{0:T(256)S(1)} %fusion.14), channel_id=1, source_target_pairs={{0,1},{1,0},{2,3},{3,2},{4,5},{5,4},{6,7},{7,6},{8,9},{9,8},{10,11... | collective-permute-start | bytes 3080 | tf_op jit(solution)/shard_map/ppermute | solution.py:29
  186.4 4.5 %collective-permute-start.39 = (f32[256]{0:T(256)S(1)}, f32[256]{0:T(256)S(1)}, u32[]{:S(2)}, u32[]{:S(2)}) collective-permute-start(f32[256]{0:T(256)S(1)} %add.203), channel_id=1, source_target_pairs={{0,2},{1,3},{2,0},{3,1},{4,6},{5,7},{6,4},{7,5},{8,10},{9,11},{10,... | collective-permute-start | bytes 3080 | tf_op jit(solution)/shard_map/ppermute | solution.py:29
  (35 other events, 409.2 us)
